TPU v7x, 128 devices: a whole 4x4x4 slice. The times are simulated.
128 devices in a mesh: row: 32 (over y, z_lo, x), col: 4 (over z_hi, core).
Axes of the slice: x: 4, y: 4, z: 4 (z_hi: 2, z_lo: 2; z = z_hi * 2 + z_lo), core: 2. Of those that a mesh axis runs over, the one named last changes fastest.
Arguments:
- ratings: bfloat16 [4, 262144, 512], P(None, ('row', 'col'))
- tile_mask: int32 [4, 2048, 4], P(None, ('row', 'col')), may hold values from 0 to 1, as said below
- tile_counts: int32 [128], replicated, may hold values from 1 to 16, as said below
- users: float32 [131072, 128], P(('row', 'col')), may hold values from -2 to 2
- user_accum: float32 [131072, 128], P(('row', 'col')), may hold values from 0.05 to 0.5
- items: float32 [65536, 128], P(('row', 'col')), may hold values from -2 to 2
- item_accum: float32 [65536, 128], P(('row', 'col')), may hold values from 0.05 to 0.5
Outputs:
- users_out: float32 [131072, 128], P(('row', 'col'))
- user_accum_out: float32 [131072, 128], P(('row', 'col'))
- items_out: float32 [65536, 128], P(('row', 'col'))
- item_accum_out: float32 [65536, 128], P(('row', 'col'))
- losses: float32 [4], replicated
Inputs may be any that keep to these rules, and one draw needn't show every extreme that they name: Each group of 4 positions has tile_counts summing to 32, and exactly one position of each group, not always the same, owns 2 * 8 tiles. `tile_mask`: in each stratum, the first slot's first item tile of every position is 1.
All inputs are finite; a program needn't handle non-finite values.
Results may differ from a plain program's by a relative error of at most 0.0025.
Values sent between devices are 32-bit elements; how exact they have to be, the bound alone decides.
No kernel may reach another device: no remote copies, remote signals or barrier semaphores. Data moves between devices by JAX's collectives and lax.ppermute only.
A program may use at most 64 MiB of HBM per device.

v0:
```python
import jax
import jax.numpy as jnp
from jax import lax
from jax.sharding import PartitionSpec as P

TILE = 128
UT = 8
STEPS = 3


ridge_weight = 0.02
step_rate = 0.05


def passed_along(value, axis, steps):
    count = lax.axis_size(axis)
    pairs = [(source, (source + steps) % count) for source in range(count)]
    return lax.ppermute(value, axis, pairs)


def update(user_fac, user_acc, item_fac, item_acc, rating_block, live_tiles):
    tile_size = user_fac.shape[0] // live_tiles.shape[0]
    user_half = user_fac.astype(jnp.bfloat16)
    item_half = item_fac.astype(jnp.bfloat16)
    predicted = lax.dot_general(
        user_half, item_half, (((1,), (1,)), ((), ())), preferred_element_type=jnp.float32
    )
    residue = predicted - rating_block.astype(jnp.float32)
    masked = (
        residue.reshape(live_tiles.shape[0], tile_size, live_tiles.shape[1], tile_size)
        * live_tiles[:, None, :, None]
    ).reshape(residue.shape)
    sq_error = jnp.sum(masked * residue)
    err_half = masked.astype(jnp.bfloat16)
    grad_user = (
        jnp.dot(err_half, item_half, preferred_element_type=jnp.float32)
        * float(item_fac.shape[0]) ** (-0.5)
        + ridge_weight * user_fac
    )
    grad_item = (
        lax.dot_general(
            err_half, user_half, (((0,), (0,)), ((), ())), preferred_element_type=jnp.float32
        )
        * float(UT * TILE) ** (-0.5)
        + ridge_weight * item_fac
    )
    user_acc = user_acc + grad_user * grad_user
    item_acc = item_acc + grad_item * grad_item
    user_fac = user_fac - step_rate * grad_user * lax.rsqrt(user_acc)
    item_fac = item_fac - step_rate * grad_item * lax.rsqrt(item_acc)
    return (user_fac, user_acc, item_fac, item_acc, sq_error)


def on_device(ratings, tile_mask, tile_counts, users, user_accum, items, item_accum):
    strata_count = ratings.shape[0]
    slot_count = tile_mask.shape[1]
    tile_size = ratings.shape[1] // slot_count
    group_size = lax.axis_size("col")
    member = lax.axis_index("col")
    arrived_rows = users.shape[0]
    group_counts = lax.dynamic_slice_in_dim(
        tile_counts, lax.axis_index("row") * group_size, group_size
    )
    ranks = jnp.arange(group_size, dtype=jnp.int32)
    start_tile = jnp.sum(jnp.where(ranks < member, group_counts, 0))
    own_count = jnp.sum(jnp.where(ranks == member, group_counts, 0))
    valid = (jnp.arange(slot_count, dtype=jnp.int32) < own_count).astype(jnp.float32)
    whole_fac, whole_acc = (
        lax.all_gather(users, "col", axis=0, tiled=True),
        lax.all_gather(user_accum, "col", axis=0, tiled=True),
    )
    pad_rows = slot_count * tile_size
    ext_fac = jnp.concatenate([whole_fac, whole_fac[:pad_rows]], axis=0)
    ext_acc = jnp.concatenate([whole_acc, whole_acc[:pad_rows]], axis=0)
    user_fac = lax.dynamic_slice_in_dim(ext_fac, start_tile * tile_size, pad_rows, 0)
    user_acc = lax.dynamic_slice_in_dim(ext_acc, start_tile * tile_size, pad_rows, 0)
    held_pair = jnp.stack([items, item_accum])
    loss_list = []
    for stratum in range(strata_count):
        live_tiles = tile_mask[stratum].astype(jnp.float32) * valid[:, None]
        item_fac = held_pair[0]
        item_acc = held_pair[1]
        for inner in range(STEPS):
            user_fac, user_acc, item_fac, item_acc, sq_error = update(
                user_fac, user_acc, item_fac, item_acc, ratings[stratum], live_tiles
            )
            if inner == 0:
                observed = jnp.sum(live_tiles) * float(tile_size * tile_size)
                total_error, total_count = lax.psum((sq_error, observed), ("row", "col"))
                loss_list.append(total_error / total_count)
        held_pair = jnp.stack([item_fac, item_acc])
        if stratum + 1 < strata_count:
            held_pair = passed_along(held_pair, ("row", "col"), 1)
    losses = jnp.stack(loss_list)
    row_valid = jnp.repeat(valid, tile_size)[:, None] > 0.5
    kept_fac = jnp.where(row_valid, user_fac, 0.0)
    kept_acc = jnp.where(row_valid, user_acc, 0.0)
    frame_rows = group_size * arrived_rows + pad_rows
    frame_fac = lax.dynamic_update_slice_in_dim(
        jnp.zeros((frame_rows, kept_fac.shape[1]), jnp.float32), kept_fac, start_tile * tile_size, 0
    )
    frame_acc = lax.dynamic_update_slice_in_dim(
        jnp.zeros((frame_rows, kept_acc.shape[1]), jnp.float32), kept_acc, start_tile * tile_size, 0
    )
    users_new, accum_new = (
        lax.psum_scatter(
            frame_fac[: group_size * arrived_rows], "col", scatter_dimension=0, tiled=True
        ),
        lax.psum_scatter(
            frame_acc[: group_size * arrived_rows], "col", scatter_dimension=0, tiled=True
        ),
    )
    return (users_new, accum_new, held_pair[0], held_pair[1], losses)


def solution(mesh):
    return jax.shard_map(
        on_device,
        mesh=mesh,
        in_specs=(
            P(None, ("row", "col"), None),
            P(None, ("row", "col"), None),
            P(),
            P(("row", "col"), None),
            P(("row", "col"), None),
            P(("row", "col"), None),
            P(("row", "col"), None),
        ),
        out_specs=(
            P(("row", "col"), None),
            P(("row", "col"), None),
            P(("row", "col"), None),
            P(("row", "col"), None),
            P(),
        ),
        check_vma=False,
    )
```

profile of v0, /device:TPU:1, one launch (start us, length us, event | category | flops | bytes accessed | tf_op | source)
XLA Modules:
  0.0 266.2 jit_solution(3098577988542652203)
XLA Ops:
  7.2 0.7 all-gather.3.cloned.1.call-update
  7.9 0.7 all-gather.5.cloned.1.call-update
  8.7 1.4 fusion.113
  10.7 0.7 compare_convert_fusion
  11.4 1.4 fusion.118
  12.9 27.1 %all-gather.3.cloned.1.call-done = f32[4096,128]{1,0:T(8,128)} async-done(((f32[1024,128]{1,0:T(8,128)}), f32[4096,128]{1,0:T(8,128)}) %all-gather.3.cloned.1.call-update) | async-done | bytes 2097168 | tf_op jit(solution)/shard_map/all_gather | solution.py:69
  40.0 1.2 slice-done.7
  41.2 1.6 fusion.37
  42.9 0.6 mul.539
  43.8 4.7 %multiply_reduce_fusion.3 = (f32[]{:T(128)}, bf16[2048,512]{1,0:T(8,128)(2,1)S(1)}) fusion(f32[256,8,4,128]{3,2,1,0:T(4,128)S(1)} %bitcast.197, bf16[4,2048,512]{2,1,0:T(8,128)(2,1)} %param.7, f32[512,128]{1,0:T(8,128)S(1)} %copy-done.8, f32[2048,128]{1,0:T(8,128)S(1)} %fusion.37), kind=kOutput, calls=%fused_computation.35 | convolution fusion | flops 275054592 | bytes 9699332 | tf_op jit(solution)/shard_map/dot_general | solution.py:25
  48.5 1.5 multiply_subtract_fusion.19
  50.0 17.7 %all-gather.5.cloned.1.call-done = f32[4096,128]{1,0:T(8,128)} async-done(((f32[1024,128]{1,0:T(8,128)}), f32[4096,128]{1,0:T(8,128)}) %all-gather.5.cloned.1.call-update) | async-done | bytes 2097168 | tf_op jit(solution)/shard_map/all_gather | solution.py:70
  67.7 1.2 slice-done.6
  68.9 2.2 multiply_subtract_fusion.10
  71.4 2.4 fusion.1
  73.8 0.8 multiply_subtract_fusion.18
  74.6 1.7 multiply_subtract_fusion.9
  76.3 2.3 fusion.3
  78.6 0.8 subtract_bitcast_fusion.2
  79.4 0.8 pad_maximum_fusion
  80.3 2.3 multiply_subtract_fusion.8
  82.7 4.0 %collective-permute-done = f32[2,512,128]{2,1,0:T(8,128)} collective-permute-done((f32[2,512,128]{2,1,0:T(8,128)}, f32[2,512,128]{2,1,0:T(8,128)}, u32[]{:S(2)}, u32[]{:S(2)}) %collective-permute-start) | collective-permute-done | bytes 524320 | tf_op jit(solution)/shard_map/ppermute | solution.py:18
  87.3 3.7 %multiply_reduce_fusion.2 = (f32[]{:T(128)}, bf16[2048,512]{1,0:T(8,128)(2,1)S(1)}) fusion(f32[256,8,4,128]{3,2,1,0:T(4,128)S(1)} %bitcast.200, bf16[4,2048,512]{2,1,0:T(8,128)(2,1)} %param.7, f32[2,512,128]{2,1,0:T(8,128)} %collective-permute-done, f32[2048,128]{1,0:T(8,128)S(1)} %get-tuple-element.33), kind=kOutput, calls=%fused_computation.34 | convolution fusion | flops 274989056 | bytes 9568260 | tf_op jit(solution)/shard_map/dot_general | solution.py:25
  91.1 1.9 multiply_subtract_fusion.17
  93.0 1.7 multiply_subtract_fusion.7
  94.7 0.7 fusion.5
  95.4 1.7 multiply_subtract_fusion.6
  97.1 1.7 multiply_subtract_fusion.16
  98.9 0.7 fusion.7
  99.6 0.7 multiply_add_fusion.22
  100.3 1.0 subtract_bitcast_fusion.1
  101.4 0.8 pad_maximum_fusion.1
  102.2 4.0 %collective-permute-start.1 = (f32[2,512,128]{2,1,0:T(8,128)}, f32[2,512,128]{2,1,0:T(8,128)}, u32[]{:S(2)}, u32[]{:S(2)}) collective-permute-start(f32[2,512,128]{2,1,0:T(8,128)} %pad_maximum_fusion.1), channel_id=1, source_target_pairs={{0,1},{1,2},{2,3},{3,4},{4,5},{5,6},{6,7},{7,8},{8,9},{9,10},{10,1... | collective-permute-start | bytes 1572872 | tf_op jit(solution)/shard_map/ppermute | solution.py:18
  106.3 0.7 broadcast_compare_fusion
  106.9 1.9 multiply_subtract_fusion.5
  108.9 3.8 %collective-permute-done.1 = f32[2,512,128]{2,1,0:T(8,128)} collective-permute-done((f32[2,512,128]{2,1,0:T(8,128)}, f32[2,512,128]{2,1,0:T(8,128)}, u32[]{:S(2)}, u32[]{:S(2)}) %collective-permute-start.1) | collective-permute-done | bytes 524320 | tf_op jit(solution)/shard_map/ppermute | solution.py:18
  112.6 0.6 mul.611
  113.2 3.7 %multiply_reduce_fusion.1 = (f32[]{:T(128)}, bf16[2048,512]{1,0:T(8,128)(2,1)S(1)}) fusion(f32[256,8,4,128]{3,2,1,0:T(4,128)S(1)} %bitcast.203, bf16[4,2048,512]{2,1,0:T(8,128)(2,1)} %param.7, f32[2,512,128]{2,1,0:T(8,128)} %collective-permute-done.1, f32[2048,128]{1,0:T(8,128)S(1)} %get-tuple-element.69), kind=kOutput, calls=%fused_computation.33 | convolution fusion | flops 274989056 | bytes 9568260 | tf_op jit(solution)/shard_map/dot_general | solution.py:25
  116.9 1.9 multiply_subtract_fusion.15
  118.9 1.7 multiply_subtract_fusion.4
  120.6 0.7 fusion.9
  121.5 1.7 multiply_subtract_fusion.3
  123.3 1.7 multiply_subtract_fusion.14
  125.0 0.7 fusion.11
  125.7 0.7 multiply_add_fusion.17
  126.5 1.0 subtract_bitcast_fusion
  127.5 0.8 pad_maximum_fusion.2
  128.3 4.0 %collective-permute-start.2 = (f32[2,512,128]{2,1,0:T(8,128)}, f32[2,512,128]{2,1,0:T(8,128)}, u32[]{:S(2)}, u32[]{:S(2)}) collective-permute-start(f32[2,512,128]{2,1,0:T(8,128)} %pad_maximum_fusion.2), channel_id=1, source_target_pairs={{0,1},{1,2},{2,3},{3,4},{4,5},{5,6},{6,7},{7,8},{8,9},{9,10},{10,1... | collective-permute-start | bytes 1572872 | tf_op jit(solution)/shard_map/ppermute | solution.py:18
  132.5 2.3 multiply_subtract_fusion.2
  134.7 7.4 %collective-permute-done.2 = f32[2,512,128]{2,1,0:T(8,128)} collective-permute-done((f32[2,512,128]{2,1,0:T(8,128)}, f32[2,512,128]{2,1,0:T(8,128)}, u32[]{:S(2)}, u32[]{:S(2)}) %collective-permute-start.2) | collective-permute-done | bytes 524320 | tf_op jit(solution)/shard_map/ppermute | solution.py:18
  142.2 0.6 mul.647
  142.8 3.7 %multiply_reduce_fusion = (f32[]{:T(128)}, bf16[2048,512]{1,0:T(8,128)(2,1)S(1)}) fusion(f32[256,8,4,128]{3,2,1,0:T(4,128)S(1)} %bitcast.206, bf16[4,2048,512]{2,1,0:T(8,128)(2,1)} %param.7, f32[2,512,128]{2,1,0:T(8,128)} %collective-permute-done.2, f32[2048,128]{1,0:T(8,128)S(1)} %get-tuple-element.27), kind=kOutput, calls=%fused_computation.32 | convolution fusion | flops 274989056 | bytes 9568260 | tf_op jit(solution)/shard_map/dot_general | solution.py:25
  146.5 1.9 multiply_subtract_fusion.13
  148.5 1.8 multiply_subtract_fusion.1
  150.3 0.7 fusion.13
  151.0 0.7 multiply_subtract_fusion
  151.7 2.4 multiply_subtract_fusion.12
  154.1 0.7 fusion.15
  155.1 0.7 select_dynamic-update-slice_fusion.1
  155.8 1.6 copy-done.5
  158.0 1.4 slice.89
  159.5 3.1 %slice.88 = f32[4096,128]{1,0:T(8,128)} slice(f32[6144,128]{1,0:T(8,128)} %copy-done.5), slice={[0:4096], [0:128]} | slice | bytes 4194304 | tf_op jit(solution)/shard_map/slice | solution.py:107
  165.2 86.0 %all-reduce = (f32[]{:T(128)}, f32[]{:T(128)}, f32[]{:T(128)}, f32[]{:T(128)}, f32[]{:T(128)}, /*index=5*/f32[]{:T(128)}, f32[]{:T(128)}, f32[]{:T(128)}) all-reduce(f32[]{:T(128)} %get-tuple-element.45, f32[]{:T(128)S(6)} %mul.689, f32[]{:T(128)} %get-tuple-element.43, ...), channel_id=1, replica_groups=mesh['row'=32,'col'=4] {'row','col'}, use_global_device_ids=true, to_apply=%region_17.18 | all-reduce | flops 8 | bytes 64 | tf_op jit(solution)/shard_map/psum | solution.py:89
  257.0 2.6 multiply_subtract_fusion.11
  (61 shorter events, 3.5 us)
Async XLA Ops:
  7.2 32.9 %all-gather.3.cloned.1.call-start = ((), (), s32[]{:S(2)}) async-start(), calls=%async_computation.2 | async-start | bytes 2621440 | tf_op jit(solution)/shard_map/all_gather | solution.py:69
  7.9 59.8 %all-gather.5.cloned.1.call-start = ((), (), s32[]{:S(2)}) async-start(), calls=%async_computation.3 | async-start | bytes 2621440 | tf_op jit(solution)/shard_map/all_gather | solution.py:70
  8.6 251.0 %reduce-scatter.5.cloned.1.call-start = ((), (), s32[]{:S(2)}) async-start(), calls=%async_computation.5 | async-start | bytes 2621440 | tf_op jit(solution)/shard_map/reduce_scatter | solution.py:109
  40.0 1.2 slice-start.7
  42.9 1.0 copy-start.8
  43.5 5.0 %copy-start = (f32[16,128,4,128]{3,2,1,0:T(4,128)}, f32[16,128,4,128]{3,2,1,0:T(4,128)S(1)}, u32[]{:S(2)}) copy-start(f32[16,128,4,128]{3,2,1,0:T(4,128)S(1)} %mul.539) | copy-start | bytes 12582916
  43.8 4.7 %copy-start.10 = (f32[512,128]{1,0:T(8,128)S(1)}, f32[512,128]{1,0:T(8,128)}, u32[]{:S(2)}) copy-start(f32[512,128]{1,0:T(8,128)} %param.13) | copy-start | bytes 786436
  67.7 1.2 slice-start.6
  67.7 1.3 copy-start.9
  68.9 2.5 copy-start.1
  71.1 3.5 %copy-start.2 = (f32[2048,128]{1,0:T(8,128)}, f32[2048,128]{1,0:T(8,128)S(1)}, u32[]{:S(2)}) copy-start(f32[2048,128]{1,0:T(8,128)S(1)} %get-tuple-element.38) | copy-start | bytes 3145732
  71.4 2.4 copy-start.11
  71.4 2.4 copy-start.12
  74.6 4.0 %copy-start.6 = (f32[512,128]{1,0:T(8,128)}, f32[512,128]{1,0:T(8,128)S(1)}, u32[]{:S(2)}) copy-start(f32[512,128]{1,0:T(8,128)S(1)} %get-tuple-element.35) | copy-start | bytes 786436
  80.2 6.5 %collective-permute-start = (f32[2,512,128]{2,1,0:T(8,128)}, f32[2,512,128]{2,1,0:T(8,128)}, u32[]{:S(2)}, u32[]{:S(2)}) collective-permute-start(f32[2,512,128]{2,1,0:T(8,128)} %pad_maximum_fusion), channel_id=1, source_target_pairs={{0,1},{1,2},{2,3},{3,4},{4,5},{5,6},{6,7},{7,8},{8,9},{9,10},{10,1... | collective-permute-start | bytes 1572872 | tf_op jit(solution)/shard_map/ppermute | solution.py:18
  87.3 7.4 %slice-start = ((s8[8388608]{0:T(1024)(128)(4,1)}), s8[4194304]{0:T(1024)(128)(4,1)S(1)}, s32[]{:S(2)}) async-start(s8[8388608]{0:T(1024)(128)(4,1)} %bitcast.191), calls=%async_computation.6 | async-start | bytes 8388608
  91.1 3.6 %slice-start.1 = ((s8[8388608]{0:T(1024)(128)(4,1)}), s8[4194304]{0:T(1024)(128)(4,1)S(1)}, s32[]{:S(2)}) async-start(s8[8388608]{0:T(1024)(128)(4,1)} %bitcast.191), calls=%async_computation.7 | async-start | bytes 8388608
  102.2 10.4 %collective-permute-start.1 = (f32[2,512,128]{2,1,0:T(8,128)}, f32[2,512,128]{2,1,0:T(8,128)}, u32[]{:S(2)}, u32[]{:S(2)}) collective-permute-start(f32[2,512,128]{2,1,0:T(8,128)} %pad_maximum_fusion.1), channel_id=1, source_target_pairs={{0,1},{1,2},{2,3},{3,4},{4,5},{5,6},{6,7},{7,8},{8,9},{9,10},{10,1... | collective-permute-start | bytes 1572872 | tf_op jit(solution)/shard_map/ppermute | solution.py:18
  113.2 7.4 %slice-start.2 = ((s8[8388608]{0:T(1024)(128)(4,1)}), s8[4194304]{0:T(1024)(128)(4,1)S(1)}, s32[]{:S(2)}) async-start(s8[8388608]{0:T(1024)(128)(4,1)} %bitcast.193), calls=%async_computation.8 | async-start | bytes 8388608
  116.9 1.9 copy-start.3
  116.9 3.7 %slice-start.3 = ((s8[8388608]{0:T(1024)(128)(4,1)}), s8[4194304]{0:T(1024)(128)(4,1)S(1)}, s32[]{:S(2)}) async-start(s8[8388608]{0:T(1024)(128)(4,1)} %bitcast.193), calls=%async_computation.9 | async-start | bytes 8388608
  120.6 1.0 copy-start.4
  128.3 13.8 %collective-permute-start.2 = (f32[2,512,128]{2,1,0:T(8,128)}, f32[2,512,128]{2,1,0:T(8,128)}, u32[]{:S(2)}, u32[]{:S(2)}) collective-permute-start(f32[2,512,128]{2,1,0:T(8,128)} %pad_maximum_fusion.2), channel_id=1, source_target_pairs={{0,1},{1,2},{2,3},{3,4},{4,5},{5,6},{6,7},{7,8},{8,9},{9,10},{10,1... | collective-permute-start | bytes 1572872 | tf_op jit(solution)/shard_map/ppermute | solution.py:18
  142.8 7.5 %slice-start.4 = ((s8[8388608]{0:T(1024)(128)(4,1)}), s8[4194304]{0:T(1024)(128)(4,1)S(1)}, s32[]{:S(2)}) async-start(s8[8388608]{0:T(1024)(128)(4,1)} %bitcast.195), calls=%async_computation.10 | async-start | bytes 8388608
  146.5 3.7 %slice-start.5 = ((s8[8388608]{0:T(1024)(128)(4,1)}), s8[4194304]{0:T(1024)(128)(4,1)S(1)}, s32[]{:S(2)}) async-start(s8[8388608]{0:T(1024)(128)(4,1)} %bitcast.195), calls=%async_computation.11 | async-start | bytes 8388608
  148.5 3.3 %copy-start.7 = (f32[512,128]{1,0:T(8,128)}, f32[512,128]{1,0:T(8,128)S(1)}, u32[]{:S(2)}) copy-start(f32[512,128]{1,0:T(8,128)S(1)} %get-tuple-element.80) | copy-start | bytes 786436
  155.8 1.6 copy-start.5
  159.5 100.2 %reduce-scatter.3.cloned.1.call-start = ((), (), s32[]{:S(2)}) async-start(), calls=%async_computation.4 | async-start | bytes 2621440 | tf_op jit(solution)/shard_map/reduce_scatter | solution.py:106
Sparse Core Ops, SparseCore 0:
  9.6 30.3 all-gather.2
  41.7 25.9 all-gather.4
  159.6 43.5 reduce-scatter.4
  206.2 37.5 reduce-scatter.2
where the time goes:
time: 268 us; the launch traced here: 266 us
  blocking collectives  86 us (32%)
  matrix products  63.9 us (24%)
  waiting for transfers between devices  61.4 us (23%)
  between operations  22.7 us (8%)
  local copies, waits for them, and re-layouts  12.8 us (5%)
  other arithmetic  11.2 us (4%)
  starting transfers between devices  8.16 us (3%)
    psum x1, blocking collectives, on_device(): total_error, total_count = lax.psum((sq_error, observed), ('row', 'col'))  86 us
    all_gather x1, waiting for transfers between devices, on_device(): lax.all_gather(users, 'col', axis=0, tiled=True)  27.1 us
    dot_general x12, matrix products, update(): lax.dot_general(user_half, item_half, (((1,), (1,)), ((), ())), preferred...  24.8 us
    dot_general x12, matrix products, update(): jnp.dot(err_half, item_half, preferred_element_type=jnp.float32)  20.4 us
    dot_general x12, matrix products, update(): lax.dot_general(err_half, user_half, (((0,), (0,)), ((), ())), preferred_...  18.7 us
    all_gather x1, waiting for transfers between devices, on_device(): lax.all_gather(user_accum, 'col', axis=0, tiled=True)  17.7 us
    ppermute x3, waiting for transfers between devices, passed_along(): return lax.ppermute(value, axis, pairs)  15.2 us
    ppermute x3, starting transfers between devices, passed_along(): return lax.ppermute(value, axis, pairs)  8.01 us
  transfers between devices with their start and end apart: 7, of which 5 were waited for; matrix products, arithmetic and copies ran while one was open for 10% of the time, Pallas kernels for 0%

commit v1 on v0

--- a/solution.py
+++ b/solution.py
@@ -65,15 +65,12 @@
     start_tile = jnp.sum(jnp.where(ranks < member, group_counts, 0))
     own_count = jnp.sum(jnp.where(ranks == member, group_counts, 0))
     valid = (jnp.arange(slot_count, dtype=jnp.int32) < own_count).astype(jnp.float32)
-    whole_fac, whole_acc = (
-        lax.all_gather(users, "col", axis=0, tiled=True),
-        lax.all_gather(user_accum, "col", axis=0, tiled=True),
-    )
+    whole_pair = lax.all_gather(jnp.stack([users, user_accum]), "col", axis=1, tiled=True)
     pad_rows = slot_count * tile_size
-    ext_fac = jnp.concatenate([whole_fac, whole_fac[:pad_rows]], axis=0)
-    ext_acc = jnp.concatenate([whole_acc, whole_acc[:pad_rows]], axis=0)
-    user_fac = lax.dynamic_slice_in_dim(ext_fac, start_tile * tile_size, pad_rows, 0)
-    user_acc = lax.dynamic_slice_in_dim(ext_acc, start_tile * tile_size, pad_rows, 0)
+    ext_pair = jnp.concatenate([whole_pair, whole_pair[:, :pad_rows]], axis=1)
+    user_pair = lax.dynamic_slice_in_dim(ext_pair, start_tile * tile_size, pad_rows, 1)
+    user_fac = user_pair[0]
+    user_acc = user_pair[1]
     held_pair = jnp.stack([items, item_accum])
     loss_list = []
     for stratum in range(strata_count):
@@ -86,31 +83,25 @@
             )
             if inner == 0:
                 observed = jnp.sum(live_tiles) * float(tile_size * tile_size)
-                total_error, total_count = lax.psum((sq_error, observed), ("row", "col"))
-                loss_list.append(total_error / total_count)
+                loss_list.append(jnp.stack([sq_error, observed]))
         held_pair = jnp.stack([item_fac, item_acc])
         if stratum + 1 < strata_count:
             held_pair = passed_along(held_pair, ("row", "col"), 1)
-    losses = jnp.stack(loss_list)
-    row_valid = jnp.repeat(valid, tile_size)[:, None] > 0.5
-    kept_fac = jnp.where(row_valid, user_fac, 0.0)
-    kept_acc = jnp.where(row_valid, user_acc, 0.0)
+    loss_parts = lax.psum(jnp.stack(loss_list), ("row", "col"))
+    losses = loss_parts[:, 0] / loss_parts[:, 1]
+    row_valid = jnp.repeat(valid, tile_size)[None, :, None] > 0.5
+    kept_pair = jnp.where(row_valid, jnp.stack([user_fac, user_acc]), 0.0)
     frame_rows = group_size * arrived_rows + pad_rows
-    frame_fac = lax.dynamic_update_slice_in_dim(
-        jnp.zeros((frame_rows, kept_fac.shape[1]), jnp.float32), kept_fac, start_tile * tile_size, 0
+    frame_pair = lax.dynamic_update_slice_in_dim(
+        jnp.zeros((2, frame_rows, kept_pair.shape[2]), jnp.float32),
+        kept_pair,
+        start_tile * tile_size,
+        1,
     )
-    frame_acc = lax.dynamic_update_slice_in_dim(
-        jnp.zeros((frame_rows, kept_acc.shape[1]), jnp.float32), kept_acc, start_tile * tile_size, 0
+    users_pair = lax.psum_scatter(
+        frame_pair[:, : group_size * arrived_rows], "col", scatter_dimension=1, tiled=True
     )
-    users_new, accum_new = (
-        lax.psum_scatter(
-            frame_fac[: group_size * arrived_rows], "col", scatter_dimension=0, tiled=True
-        ),
-        lax.psum_scatter(
-            frame_acc[: group_size * arrived_rows], "col", scatter_dimension=0, tiled=True
-        ),
-    )
-    return (users_new, accum_new, held_pair[0], held_pair[1], losses)
+    return (users_pair[0], users_pair[1], held_pair[0], held_pair[1], losses)
 
 
 def solution(mesh):

time: 268 us -> 257 us (0.959)
  matrix products: 63.9 us -> 56 us
  blocking collectives: 86 us -> 93.7 us
  waiting for transfers between devices: 61.4 us -> 55.2 us
  between operations: 22.7 us -> 17.7 us
  other arithmetic: 11.2 us -> 15 us
    psum x1, blocking collectives: 86 us -> 93.7 us  [on_device(): loss_parts = lax.psum(jnp.stack(loss_list), ('row', 'col'))]
    dot_general x12, matrix products: 24.8 us -> 18.6 us  [update(): lax.dot_general(user_half, item_half, (((1,), (1,)), ((), ())), preferred...]
    all_gather x2 -> x1, waiting for transfers between devices: 44.8 us -> 39.6 us  [on_device(): lax.all_gather(jnp.stack([users, user_accum]), 'col', axis=1, tiled=True)]
    another operation x1 -> x6, other arithmetic: 0.59 us -> 5.05 us  [the longest x5 2.78 us: on_device(): loss_parts = lax.psum(jnp.stack(loss_list), ('row', 'col'))]
    slice x6 -> x2, local copies, waits for them, and re-layouts: 6.97 us -> 4.1 us  [the longest x1 2.22 us: on_device(): frame_pair[:, :group_size * arrived_rows]]
  transfers between devices with their start and end apart: 7 -> 5, of which waited for: 5 -> 4; matrix products, arithmetic and copies ran while one was open for 10% -> 6% of each run, Pallas kernels for 0% -> 0%
where the time goes in v1:
time: 257 us
  blocking collectives  93.7 us (36%)
  matrix products  56 us (22%)
  waiting for transfers between devices  55.2 us (21%)
  between operations  17.7 us (7%)
  other arithmetic  15 us (6%)
  local copies, waits for them, and re-layouts  10.8 us (4%)
  starting transfers between devices  8.1 us (3%)
    psum x1, blocking collectives, on_device(): loss_parts = lax.psum(jnp.stack(loss_list), ('row', 'col'))  93.7 us
    all_gather x1, waiting for transfers between devices, on_device(): lax.all_gather(jnp.stack([users, user_accum]), 'col', axis=1, tiled=True)  39.6 us
    dot_general x12, matrix products, update(): jnp.dot(err_half, item_half, preferred_element_type=jnp.float32)  19.3 us
    dot_general x12, matrix products, update(): lax.dot_general(user_half, item_half, (((1,), (1,)), ((), ())), preferred...  18.6 us
    dot_general x12, matrix products, update(): lax.dot_general(err_half, user_half, (((0,), (0,)), ((), ())), preferred_...  18.1 us
    ppermute x3, waiting for transfers between devices, passed_along(): return lax.ppermute(value, axis, pairs)  15.6 us
    ppermute x3, starting transfers between devices, passed_along(): return lax.ppermute(value, axis, pairs)  8.02 us
  transfers between devices with their start and end apart: 5, of which 4 were waited for; matrix products, arithmetic and copies ran while one was open for 6% of the time, Pallas kernels for 0%

profile of v1, /device:TPU:1, one launch (start us, length us, event | category | flops | bytes accessed | tf_op | source)
XLA Modules:
  0.0 256.5 jit_solution(1015268047695154100)
XLA Ops:
  7.2 2.3 pad_maximum_fusion
  9.6 0.7 fusion.116
  11.0 0.7 compare_convert_fusion
  11.6 0.7 fusion.121
  12.4 39.6 %all-gather.2.cloned.1.call-done = f32[2,4096,128]{2,1,0:T(8,128)} async-done(((f32[2,1024,128]{2,1,0:T(8,128)}), f32[2,4096,128]{2,1,0:T(8,128)}) %all-gather.2.cloned.1.call-update) | async-done | bytes 4194320 | tf_op jit(solution)/shard_map/all_gather | solution.py:68
  51.9 1.9 slice.96
  53.8 2.2 fusion.32
  56.0 0.6 mul.537
  57.4 1.9 multiply_reduce_fusion.3
  59.3 0.7 multiply_subtract_fusion.10
  60.2 0.8 multiply_subtract_fusion.19
  61.0 0.7 fusion.1
  61.7 0.8 multiply_subtract_fusion.18
  62.5 1.7 multiply_subtract_fusion.9
  64.2 0.7 fusion.3
  64.9 0.8 subtract_bitcast_fusion.3
  65.7 0.8 pad_maximum_fusion.1
  66.6 2.6 %multiply_subtract_fusion.8 = (f32[2048,128]{1,0:T(8,128)S(1)}, f32[2048,128]{1,0:T(8,128)S(1)}) fusion(f32[2048,128]{1,0:T(8,128)S(1)} %get-tuple-element.57, f32[2048,128]{1,0:T(8,128)} %get-tuple-element.58, f32[2048,128]{1,0:T(8,128)} %copy-done.1, f32[2,2048,128]{2,1,0:T(8,128)} %copy-done, bf16[2048,512]{1,0:T(8,128)(2,1)S(1)} %fusion.3, ...), kind=kOutput, calls=%fused_computation.106 | convolution fusion | flops 271646720 | bytes 8650752 | tf_op jit(solution)/shard_map/dot_general | solution.py:36
  69.2 3.8 %collective-permute-done = f32[2,512,128]{2,1,0:T(8,128)} collective-permute-done((f32[2,512,128]{2,1,0:T(8,128)}, f32[2,512,128]{2,1,0:T(8,128)}, u32[]{:S(2)}, u32[]{:S(2)}) %collective-permute-start) | collective-permute-done | bytes 524320 | tf_op jit(solution)/shard_map/ppermute | solution.py:18
  73.0 0.6 mul.573
  73.6 3.7 %multiply_reduce_fusion.2 = (f32[]{:T(128)}, bf16[2048,512]{1,0:T(8,128)(2,1)S(1)}) fusion(f32[256,8,4,128]{3,2,1,0:T(4,128)S(1)} %bitcast.246, bf16[4,2048,512]{2,1,0:T(8,128)(2,1)} %param.7, f32[2,512,128]{2,1,0:T(8,128)} %collective-permute-done, f32[2048,128]{1,0:T(8,128)S(1)} %get-tuple-element.25), kind=kOutput, calls=%fused_computation.36 | convolution fusion | flops 274989056 | bytes 9568260 | tf_op jit(solution)/shard_map/dot_general | solution.py:25
  77.4 1.9 multiply_subtract_fusion.17
  79.3 1.7 multiply_subtract_fusion.7
  81.0 0.7 fusion.5
  81.7 1.7 multiply_subtract_fusion.6
  83.5 1.7 multiply_subtract_fusion.16
  85.2 0.7 fusion.7
  85.9 0.7 multiply_add_fusion.22
  86.6 1.0 subtract_bitcast_fusion.2
  87.7 0.8 pad_maximum_fusion.2
  88.5 4.0 %collective-permute-start.1 = (f32[2,512,128]{2,1,0:T(8,128)}, f32[2,512,128]{2,1,0:T(8,128)}, u32[]{:S(2)}, u32[]{:S(2)}) collective-permute-start(f32[2,512,128]{2,1,0:T(8,128)} %pad_maximum_fusion.2), channel_id=1, source_target_pairs={{0,1},{1,2},{2,3},{3,4},{4,5},{5,6},{6,7},{7,8},{8,9},{9,10},{10,1... | collective-permute-start | bytes 1572872 | tf_op jit(solution)/shard_map/ppermute | solution.py:18
  92.6 1.9 multiply_subtract_fusion.5
  94.5 4.4 %collective-permute-done.1 = f32[2,512,128]{2,1,0:T(8,128)} collective-permute-done((f32[2,512,128]{2,1,0:T(8,128)}, f32[2,512,128]{2,1,0:T(8,128)}, u32[]{:S(2)}, u32[]{:S(2)}) %collective-permute-start.1) | collective-permute-done | bytes 524320 | tf_op jit(solution)/shard_map/ppermute | solution.py:18
  99.6 3.7 %multiply_reduce_fusion.1 = (f32[]{:T(128)}, bf16[2048,512]{1,0:T(8,128)(2,1)S(1)}) fusion(f32[256,8,4,128]{3,2,1,0:T(4,128)S(1)} %bitcast.249, bf16[4,2048,512]{2,1,0:T(8,128)(2,1)} %param.7, f32[2,512,128]{2,1,0:T(8,128)} %collective-permute-done.1, f32[2048,128]{1,0:T(8,128)S(1)} %get-tuple-element.65), kind=kOutput, calls=%fused_computation.35 | convolution fusion | flops 274989056 | bytes 9568260 | tf_op jit(solution)/shard_map/dot_general | solution.py:25
  103.3 1.9 multiply_subtract_fusion.15
  105.2 1.7 multiply_subtract_fusion.4
  106.9 0.7 fusion.9
  107.9 1.8 multiply_subtract_fusion.3
  109.6 1.7 multiply_subtract_fusion.14
  111.3 0.7 fusion.11
  112.1 0.7 multiply_add_fusion.17
  112.8 1.0 subtract_bitcast_fusion.1
  113.9 0.8 pad_maximum_fusion.3
  114.7 4.0 %collective-permute-start.2 = (f32[2,512,128]{2,1,0:T(8,128)}, f32[2,512,128]{2,1,0:T(8,128)}, u32[]{:S(2)}, u32[]{:S(2)}) collective-permute-start(f32[2,512,128]{2,1,0:T(8,128)} %pad_maximum_fusion.3), channel_id=1, source_target_pairs={{0,1},{1,2},{2,3},{3,4},{4,5},{5,6},{6,7},{7,8},{8,9},{9,10},{10,1... | collective-permute-start | bytes 1572872 | tf_op jit(solution)/shard_map/ppermute | solution.py:18
  118.8 2.3 multiply_subtract_fusion.2
  121.1 7.4 %collective-permute-done.2 = f32[2,512,128]{2,1,0:T(8,128)} collective-permute-done((f32[2,512,128]{2,1,0:T(8,128)}, f32[2,512,128]{2,1,0:T(8,128)}, u32[]{:S(2)}, u32[]{:S(2)}) %collective-permute-start.2) | collective-permute-done | bytes 524320 | tf_op jit(solution)/shard_map/ppermute | solution.py:18
  128.5 0.6 mul.645
  129.1 3.7 %multiply_reduce_fusion = (f32[]{:T(128)}, bf16[2048,512]{1,0:T(8,128)(2,1)S(1)}) fusion(f32[256,8,4,128]{3,2,1,0:T(4,128)S(1)} %bitcast.252, bf16[4,2048,512]{2,1,0:T(8,128)(2,1)} %param.7, f32[2,512,128]{2,1,0:T(8,128)} %collective-permute-done.2, f32[2048,128]{1,0:T(8,128)S(1)} %get-tuple-element.19), kind=kOutput, calls=%fused_computation.34 | convolution fusion | flops 274989056 | bytes 9568260 | tf_op jit(solution)/shard_map/dot_general | solution.py:25
  132.8 1.9 multiply_subtract_fusion.13
  134.8 1.8 multiply_subtract_fusion.1
  136.6 0.7 fusion.13
  137.3 0.8 multiply_subtract_fusion
  138.0 2.4 multiply_subtract_fusion.12
  140.5 0.7 fusion.15
  141.2 0.7 subtract_bitcast_fusion
  142.8 2.2 slice.105
  147.6 0.7 maximum_bitcast_fusion
  148.3 0.7 maximum_bitcast_fusion.1
  149.0 0.6 maximum_bitcast_fusion.2
  149.6 0.7 maximum_bitcast_fusion.3
  150.4 93.7 %psum.7 = f32[4,2]{1,0:T(4,128)S(1)} all-reduce(f32[4,2]{1,0:T(4,128)S(1)} %pad_maximum_fusion.4), channel_id=1, replica_groups=mesh['row'=32,'col'=4] {'row','col'}, use_global_device_ids=true, to_apply=%region_11.12 | all-reduce | flops 8 | bytes 64 | tf_op jit(solution)/shard_map/psum | solution.py:90
  244.1 0.7 fusion.115
  244.8 2.6 %multiply_subtract_fusion.11 = (f32[512,128]{1,0:T(8,128)}, f32[512,128]{1,0:T(8,128)}) fusion(f32[512,128]{1,0:T(8,128)S(1)} %get-tuple-element.77, f32[512,128]{1,0:T(8,128)} %get-tuple-element.78, f32[512,128]{1,0:T(8,128)} %copy-done.4, f32[2,512,128]{2,1,0:T(8,128)} %collective-permute-done.2, bf16[2048,512]{1,0:T(8,128)(2,1)S(1)} %fusion.15, ...), kind=kOutput, calls=%fused_computation.127 | convolution fusion | flops 269484032 | bytes 4718592 | tf_op jit(solution)/shard_map/dot_general | solution.py:41
  247.4 2.2 slice_bitcast_fusion.2
  (53 shorter events, 3.3 us)
Async XLA Ops:
  7.2 2.4 copy-start.8
  7.2 4.4 %copy-start.7 = (s32[4,16,4]{1,2,0:T(4,128)S(1)}, s32[4,16,4]{1,2,0:T(4,128)}, u32[]{:S(2)}) copy-start(s32[4,16,4]{1,2,0:T(4,128)} %param.8) | copy-start | bytes 3076
  7.2 44.8 %all-gather.2.cloned.1.call-start = ((), (), s32[]{:S(2)}) async-start(), calls=%async_computation.1 | async-start | bytes 5242880 | tf_op jit(solution)/shard_map/all_gather | solution.py:68
  9.5 237.9 %reduce-scatter.2.cloned.1.call-start = ((), (), s32[]{:S(2)}) async-start(), calls=%async_computation.2 | async-start | bytes 5242880 | tf_op jit(solution)/shard_map/reduce_scatter | solution.py:101
  51.9 4.7 %slice-start = ((s8[8388608]{0:T(1024)(128)(4,1)}), s8[4194304]{0:T(1024)(128)(4,1)S(1)}, s32[]{:S(2)}) async-start(s8[8388608]{0:T(1024)(128)(4,1)} %bitcast.238), calls=%async_computation.3 | async-start | bytes 8388608
  53.8 3.1 %slice-start.1 = ((s8[8388608]{0:T(1024)(128)(4,1)}), s8[4194304]{0:T(1024)(128)(4,1)S(1)}, s32[]{:S(2)}) async-start(s8[8388608]{0:T(1024)(128)(4,1)} %bitcast.238), calls=%async_computation.4 | async-start | bytes 8388608
  56.0 6.5 %copy-start = (f32[2,2048,128]{2,1,0:T(8,128)}, f32[2,2048,128]{2,1,0:T(8,128)S(1)}, u32[]{:S(2)}) copy-start(f32[2,2048,128]{2,1,0:T(8,128)S(1)} %fusion.32) | copy-start | bytes 6291460
  56.0 1.4 copy-start.5
  59.3 0.9 copy-start.6
  60.2 2.3 copy-start.1
  66.5 6.5 %collective-permute-start = (f32[2,512,128]{2,1,0:T(8,128)}, f32[2,512,128]{2,1,0:T(8,128)}, u32[]{:S(2)}, u32[]{:S(2)}) collective-permute-start(f32[2,512,128]{2,1,0:T(8,128)} %pad_maximum_fusion.1), channel_id=1, source_target_pairs={{0,1},{1,2},{2,3},{3,4},{4,5},{5,6},{6,7},{7,8},{8,9},{9,10},{10,1... | collective-permute-start | bytes 1572872 | tf_op jit(solution)/shard_map/ppermute | solution.py:18
  73.6 7.4 %slice-start.2 = ((s8[8388608]{0:T(1024)(128)(4,1)}), s8[4194304]{0:T(1024)(128)(4,1)S(1)}, s32[]{:S(2)}) async-start(s8[8388608]{0:T(1024)(128)(4,1)} %bitcast.240), calls=%async_computation.5 | async-start | bytes 8388608
  77.4 3.6 %slice-start.3 = ((s8[8388608]{0:T(1024)(128)(4,1)}), s8[4194304]{0:T(1024)(128)(4,1)S(1)}, s32[]{:S(2)}) async-start(s8[8388608]{0:T(1024)(128)(4,1)} %bitcast.240), calls=%async_computation.6 | async-start | bytes 8388608
  88.5 10.4 %collective-permute-start.1 = (f32[2,512,128]{2,1,0:T(8,128)}, f32[2,512,128]{2,1,0:T(8,128)}, u32[]{:S(2)}, u32[]{:S(2)}) collective-permute-start(f32[2,512,128]{2,1,0:T(8,128)} %pad_maximum_fusion.2), channel_id=1, source_target_pairs={{0,1},{1,2},{2,3},{3,4},{4,5},{5,6},{6,7},{7,8},{8,9},{9,10},{10,1... | collective-permute-start | bytes 1572872 | tf_op jit(solution)/shard_map/ppermute | solution.py:18
  99.6 7.4 %slice-start.4 = ((s8[8388608]{0:T(1024)(128)(4,1)}), s8[4194304]{0:T(1024)(128)(4,1)S(1)}, s32[]{:S(2)}) async-start(s8[8388608]{0:T(1024)(128)(4,1)} %bitcast.242), calls=%async_computation.7 | async-start | bytes 8388608
  103.3 1.9 copy-start.2
  103.3 3.7 %slice-start.5 = ((s8[8388608]{0:T(1024)(128)(4,1)}), s8[4194304]{0:T(1024)(128)(4,1)S(1)}, s32[]{:S(2)}) async-start(s8[8388608]{0:T(1024)(128)(4,1)} %bitcast.242), calls=%async_computation.8 | async-start | bytes 8388608
  106.9 0.9 copy-start.3
  114.7 13.8 %collective-permute-start.2 = (f32[2,512,128]{2,1,0:T(8,128)}, f32[2,512,128]{2,1,0:T(8,128)}, u32[]{:S(2)}, u32[]{:S(2)}) collective-permute-start(f32[2,512,128]{2,1,0:T(8,128)} %pad_maximum_fusion.3), channel_id=1, source_target_pairs={{0,1},{1,2},{2,3},{3,4},{4,5},{5,6},{6,7},{7,8},{8,9},{9,10},{10,1... | collective-permute-start | bytes 1572872 | tf_op jit(solution)/shard_map/ppermute | solution.py:18
  129.1 7.4 %slice-start.6 = ((s8[8388608]{0:T(1024)(128)(4,1)}), s8[4194304]{0:T(1024)(128)(4,1)S(1)}, s32[]{:S(2)}) async-start(s8[8388608]{0:T(1024)(128)(4,1)} %bitcast.244), calls=%async_computation.9 | async-start | bytes 8388608
  132.8 3.7 %slice-start.7 = ((s8[8388608]{0:T(1024)(128)(4,1)}), s8[4194304]{0:T(1024)(128)(4,1)S(1)}, s32[]{:S(2)}) async-start(s8[8388608]{0:T(1024)(128)(4,1)} %bitcast.244), calls=%async_computation.10 | async-start | bytes 8388608
  134.7 3.3 %copy-start.4 = (f32[512,128]{1,0:T(8,128)}, f32[512,128]{1,0:T(8,128)S(1)}, u32[]{:S(2)}) copy-start(f32[512,128]{1,0:T(8,128)S(1)} %get-tuple-element.76) | copy-start | bytes 786436
Sparse Core Ops, SparseCore 0:
  9.7 42.2 all-gather.1
  145.1 56.8 reduce-scatter.1

commit v2 on v1

--- a/solution.py
+++ b/solution.py
@@ -16,6 +16,18 @@
     count = lax.axis_size(axis)
     pairs = [(source, (source + steps) % count) for source in range(count)]
     return lax.ppermute(value, axis, pairs)
+
+
+def butterfly_sum(value, axis):
+    count = lax.axis_size(axis)
+    if count & (count - 1):
+        return lax.psum(value, axis)
+    stride = 1
+    while stride < count:
+        pairs = [(source, source ^ stride) for source in range(count)]
+        value = value + lax.ppermute(value, axis, pairs)
+        stride *= 2
+    return value
 
 
 def update(user_fac, user_acc, item_fac, item_acc, rating_block, live_tiles):
@@ -87,7 +99,7 @@
         held_pair = jnp.stack([item_fac, item_acc])
         if stratum + 1 < strata_count:
             held_pair = passed_along(held_pair, ("row", "col"), 1)
-    loss_parts = lax.psum(jnp.stack(loss_list), ("row", "col"))
+    loss_parts = butterfly_sum(jnp.stack(loss_list), ("row", "col"))
     losses = loss_parts[:, 0] / loss_parts[:, 1]
     row_valid = jnp.repeat(valid, tile_size)[None, :, None] > 0.5
     kept_pair = jnp.where(row_valid, jnp.stack([user_fac, user_acc]), 0.0)

time: 257 us -> 211 us (0.82)
  blocking collectives: 93.7 us -> 0 us
  waiting for transfers between devices: 55.2 us -> 90.4 us
  starting transfers between devices: 8.1 us -> 21 us
    psum x1 -> x0, blocking collectives: 93.7 us -> none  [on_device(): loss_parts = lax.psum(jnp.stack(loss_list), ('row', 'col'))]
    ppermute x0 -> x7, waiting for transfers between devices: none -> 20.5 us  [butterfly_sum(): value = value + lax.ppermute(value, axis, pairs)]
    reduce_scatter x1, waiting for transfers between devices: 0.01 us -> 14.8 us  [on_device(): lax.psum_scatter(frame_pair[:, :group_size * arrived_rows], 'col', scatte...]
    ppermute x0 -> x7, starting transfers between devices: none -> 12.9 us  [butterfly_sum(): value = value + lax.ppermute(value, axis, pairs)]
  transfers between devices with their start and end apart: 5 -> 12, of which waited for: 4 -> 11; matrix products, arithmetic and copies ran while one was open for 6% -> 7% of each run, Pallas kernels for 0% -> 0%
where the time goes in v2:
time: 211 us
  waiting for transfers between devices  90.4 us (43%)
  matrix products  55.9 us (26%)
  starting transfers between devices  21 us (10%)
  between operations  17.7 us (8%)
  other arithmetic  15 us (7%)
  local copies, waits for them, and re-layouts  10.8 us (5%)
    all_gather x1, waiting for transfers between devices, on_device(): lax.all_gather(jnp.stack([users, user_accum]), 'col', axis=1, tiled=True)  39.5 us
    ppermute x7, waiting for transfers between devices, butterfly_sum(): value = value + lax.ppermute(value, axis, pairs)  20.5 us
    dot_general x12, matrix products, update(): jnp.dot(err_half, item_half, preferred_element_type=jnp.float32)  19.2 us
    dot_general x12, matrix products, update(): lax.dot_general(user_half, item_half, (((1,), (1,)), ((), ())), preferred...  18.6 us
    dot_general x12, matrix products, update(): lax.dot_general(err_half, user_half, (((0,), (0,)), ((), ())), preferred_...  18.1 us
    ppermute x3, waiting for transfers between devices, passed_along(): return lax.ppermute(value, axis, pairs)  15.6 us
    reduce_scatter x1, waiting for transfers between devices, on_device(): lax.psum_scatter(frame_pair[:, :group_size * arrived_rows], 'col', scatte...  14.8 us
    ppermute x7, starting transfers between devices, butterfly_sum(): value = value + lax.ppermute(value, axis, pairs)  12.9 us
  transfers between devices with their start and end apart: 12, of which 11 were waited for; matrix products, arithmetic and copies ran while one was open for 7% of the time, Pallas kernels for 0%

profile of v2, /device:TPU:1, one launch (start us, length us, event | category | flops | bytes accessed | tf_op | source)
XLA Modules:
  0.0 210.9 jit_solution(9835630338020417176)
XLA Ops:
  7.2 2.3 %pad_maximum_fusion = f32[2,1024,128]{2,1,0:T(8,128)} fusion(f32[1,1024,128]{2,1,0:T(8,128)} %bitcast.258, f32[1,1024,128]{2,1,0:T(8,128)} %bitcast.259), kind=kLoop, calls=%fused_computation.87 | loop fusion | flops 262144 | bytes 2097152 | tf_op jit(solution)/shard_map/stack | solution.py:80
  9.6 0.7 fusion.116
  12.4 39.5 %all-gather.2.cloned.1.call-done = f32[2,4096,128]{2,1,0:T(8,128)} async-done(((f32[2,1024,128]{2,1,0:T(8,128)}), f32[2,4096,128]{2,1,0:T(8,128)}) %all-gather.2.cloned.1.call-update) | async-done | bytes 4194320 | tf_op jit(solution)/shard_map/all_gather | solution.py:80
  52.0 1.9 slice.96
  53.8 2.2 %fusion.32 = f32[2,2048,128]{2,1,0:T(8,128)S(1)} fusion(s32[]{:T(128)S(6)} %select_n.21, f32[2,4096,128]{2,1,0:T(8,128)} %all-gather.2.cloned.1.call-done, f32[2,2048,128]{2,1,0:T(8,128)S(1)} %slice.96), kind=kLoop, calls=%fused_computation.66 | loop fusion | flops 524288 | bytes 8388612 | tf_op jit(solution)/shard_map/concatenate | solution.py:82
  57.4 1.8 multiply_reduce_fusion.3
  59.2 0.7 multiply_subtract_fusion.10
  60.2 0.8 multiply_subtract_fusion.19
  60.9 0.7 fusion.1
  61.6 0.8 multiply_subtract_fusion.18
  62.4 1.7 multiply_subtract_fusion.9
  64.2 0.7 fusion.3
  64.9 0.8 subtract_bitcast_fusion.3
  65.6 0.8 pad_maximum_fusion.1
  66.6 2.6 %multiply_subtract_fusion.8 = (f32[2048,128]{1,0:T(8,128)S(1)}, f32[2048,128]{1,0:T(8,128)S(1)}) fusion(f32[2048,128]{1,0:T(8,128)S(1)} %get-tuple-element.57, f32[2048,128]{1,0:T(8,128)} %get-tuple-element.58, f32[2048,128]{1,0:T(8,128)} %copy-done.1, f32[2,2048,128]{2,1,0:T(8,128)} %copy-done, bf16[2048,512]{1,0:T(8,128)(2,1)S(1)} %fusion.3, ...), kind=kOutput, calls=%fused_computation.106 | convolution fusion | flops 271646720 | bytes 8650752 | tf_op jit(solution)/shard_map/dot_general | solution.py:48
  69.2 3.8 %collective-permute-done = f32[2,512,128]{2,1,0:T(8,128)} collective-permute-done((f32[2,512,128]{2,1,0:T(8,128)}, f32[2,512,128]{2,1,0:T(8,128)}, u32[]{:S(2)}, u32[]{:S(2)}) %collective-permute-start) | collective-permute-done | bytes 524320 | tf_op jit(solution)/shard_map/ppermute | solution.py:18
  73.6 3.7 %multiply_reduce_fusion.2 = (f32[]{:T(128)}, bf16[2048,512]{1,0:T(8,128)(2,1)S(1)}) fusion(f32[256,8,4,128]{3,2,1,0:T(4,128)S(1)} %bitcast.246, bf16[4,2048,512]{2,1,0:T(8,128)(2,1)} %param.7, f32[2,512,128]{2,1,0:T(8,128)} %collective-permute-done, f32[2048,128]{1,0:T(8,128)S(1)} %get-tuple-element.25), kind=kOutput, calls=%fused_computation.36 | convolution fusion | flops 274989056 | bytes 9568260 | tf_op jit(solution)/shard_map/dot_general | solution.py:37
  77.3 1.9 multiply_subtract_fusion.17
  79.2 1.7 multiply_subtract_fusion.7
  80.9 0.7 fusion.5
  81.6 1.7 multiply_subtract_fusion.6
  83.3 1.7 multiply_subtract_fusion.16
  85.0 0.7 fusion.7
  85.8 0.7 multiply_add_fusion.22
  86.5 1.0 subtract_bitcast_fusion.2
  87.6 0.8 pad_maximum_fusion.2
  88.4 4.0 %collective-permute-start.1 = (f32[2,512,128]{2,1,0:T(8,128)}, f32[2,512,128]{2,1,0:T(8,128)}, u32[]{:S(2)}, u32[]{:S(2)}) collective-permute-start(f32[2,512,128]{2,1,0:T(8,128)} %pad_maximum_fusion.2), channel_id=1, source_target_pairs={{0,1},{1,2},{2,3},{3,4},{4,5},{5,6},{6,7},{7,8},{8,9},{9,10},{10,1... | collective-permute-start | bytes 1572872 | tf_op jit(solution)/shard_map/ppermute | solution.py:18
  92.5 1.9 multiply_subtract_fusion.5
  94.4 4.4 %collective-permute-done.1 = f32[2,512,128]{2,1,0:T(8,128)} collective-permute-done((f32[2,512,128]{2,1,0:T(8,128)}, f32[2,512,128]{2,1,0:T(8,128)}, u32[]{:S(2)}, u32[]{:S(2)}) %collective-permute-start.1) | collective-permute-done | bytes 524320 | tf_op jit(solution)/shard_map/ppermute | solution.py:18
  99.4 3.7 %multiply_reduce_fusion.1 = (f32[]{:T(128)}, bf16[2048,512]{1,0:T(8,128)(2,1)S(1)}) fusion(f32[256,8,4,128]{3,2,1,0:T(4,128)S(1)} %bitcast.249, bf16[4,2048,512]{2,1,0:T(8,128)(2,1)} %param.7, f32[2,512,128]{2,1,0:T(8,128)} %collective-permute-done.1, f32[2048,128]{1,0:T(8,128)S(1)} %get-tuple-element.65), kind=kOutput, calls=%fused_computation.35 | convolution fusion | flops 274989056 | bytes 9568260 | tf_op jit(solution)/shard_map/dot_general | solution.py:37
  103.1 1.9 multiply_subtract_fusion.15
  105.1 1.7 multiply_subtract_fusion.4
  106.8 0.7 fusion.9
  107.8 1.7 multiply_subtract_fusion.3
  109.5 1.7 multiply_subtract_fusion.14
  111.2 0.7 fusion.11
  111.9 0.7 multiply_add_fusion.17
  112.7 1.0 subtract_bitcast_fusion.1
  113.7 0.8 pad_maximum_fusion.3
  114.6 4.0 %collective-permute-start.2 = (f32[2,512,128]{2,1,0:T(8,128)}, f32[2,512,128]{2,1,0:T(8,128)}, u32[]{:S(2)}, u32[]{:S(2)}) collective-permute-start(f32[2,512,128]{2,1,0:T(8,128)} %pad_maximum_fusion.3), channel_id=1, source_target_pairs={{0,1},{1,2},{2,3},{3,4},{4,5},{5,6},{6,7},{7,8},{8,9},{9,10},{10,1... | collective-permute-start | bytes 1572872 | tf_op jit(solution)/shard_map/ppermute | solution.py:18
  118.7 2.3 %multiply_subtract_fusion.2 = (f32[2048,128]{1,0:T(8,128)S(1)}, f32[2048,128]{1,0:T(8,128)S(1)}) fusion(f32[2048,128]{1,0:T(8,128)S(1)} %get-tuple-element.69, f32[2048,128]{1,0:T(8,128)} %copy-done.3, f32[2048,128]{1,0:T(8,128)} %get-tuple-element.70, bf16[2048,512]{1,0:T(8,128)(2,1)S(1)} %fusion.11, f32[512,128]{1,0:T(8,128)S(1)} %get-tuple-element.71), kind=kOutput, calls=%fused_computation.94 | convolution fusion | flops 271122432 | bytes 7602176 | tf_op jit(solution)/shard_map/dot_general | solution.py:48
  121.0 7.4 %collective-permute-done.2 = f32[2,512,128]{2,1,0:T(8,128)} collective-permute-done((f32[2,512,128]{2,1,0:T(8,128)}, f32[2,512,128]{2,1,0:T(8,128)}, u32[]{:S(2)}, u32[]{:S(2)}) %collective-permute-start.2) | collective-permute-done | bytes 524320 | tf_op jit(solution)/shard_map/ppermute | solution.py:18
  129.0 3.7 %multiply_reduce_fusion = (f32[]{:T(128)}, bf16[2048,512]{1,0:T(8,128)(2,1)S(1)}) fusion(f32[256,8,4,128]{3,2,1,0:T(4,128)S(1)} %bitcast.252, bf16[4,2048,512]{2,1,0:T(8,128)(2,1)} %param.7, f32[2,512,128]{2,1,0:T(8,128)} %collective-permute-done.2, f32[2048,128]{1,0:T(8,128)S(1)} %get-tuple-element.19), kind=kOutput, calls=%fused_computation.34 | convolution fusion | flops 274989056 | bytes 9568260 | tf_op jit(solution)/shard_map/dot_general | solution.py:37
  132.7 1.9 multiply_subtract_fusion.13
  134.6 1.8 multiply_subtract_fusion.1
  136.4 0.7 fusion.13
  137.1 0.8 multiply_subtract_fusion
  137.9 2.4 %multiply_subtract_fusion.12 = (f32[512,128]{1,0:T(8,128)S(1)}, f32[512,128]{1,0:T(8,128)}) fusion(f32[512,128]{1,0:T(8,128)S(1)} %get-tuple-element.75, f32[512,128]{1,0:T(8,128)S(1)} %get-tuple-element.76, f32[2,512,128]{2,1,0:T(8,128)} %collective-permute-done.2, bf16[2048,512]{1,0:T(8,128)(2,1)S(1)} %fusion.13, f32[2048,128]{1,0:T(8,128)S(1)} %get-tuple-element.73), kind=kOutput, calls=%fused_computation.130 | convolution fusion | flops 269352960 | bytes 4456448 | tf_op jit(solution)/shard_map/dot_general | solution.py:53
  140.3 0.7 fusion.15
  141.0 0.7 subtract_bitcast_fusion
  142.6 2.2 %slice.105 = f32[2,4096,128]{2,1,0:T(8,128)} slice(f32[2,6144,128]{2,1,0:T(8,128)S(1)} %fusion.33), slice={[0:2], [0:4096], [0:128]} | slice | bytes 8388608 | tf_op jit(solution)/shard_map/slice | solution.py:114
  148.8 0.7 maximum_bitcast_fusion.2
  149.5 0.7 maximum_bitcast_fusion.3
  150.2 12.7 %collective-permute-start.3 = (f32[4,2]{1,0:T(4,128)S(1)}, f32[4,2]{1,0:T(4,128)S(1)}, u32[]{:S(2)}, u32[]{:S(2)}) collective-permute-start(f32[4,2]{1,0:T(4,128)S(1)} %pad_maximum_fusion.4), channel_id=1, source_target_pairs={{0,1},{1,0},{2,3},{3,2},{4,5},{5,4},{6,7},{7,6},{8,9},{9,8},{10,11... | collective-permute-start | bytes 104 | tf_op jit(solution)/shard_map/ppermute | solution.py:28
  162.9 2.7 %multiply_subtract_fusion.11 = (f32[512,128]{1,0:T(8,128)}, f32[512,128]{1,0:T(8,128)}) fusion(f32[512,128]{1,0:T(8,128)S(1)} %get-tuple-element.77, f32[512,128]{1,0:T(8,128)} %get-tuple-element.78, f32[512,128]{1,0:T(8,128)} %copy-done.4, f32[2,512,128]{2,1,0:T(8,128)} %collective-permute-done.2, bf16[2048,512]{1,0:T(8,128)(2,1)S(1)} %fusion.15, ...), kind=kOutput, calls=%fused_computation.127 | convolution fusion | flops 269484032 | bytes 4718592 | tf_op jit(solution)/shard_map/dot_general | solution.py:53
  165.7 3.9 %collective-permute-done.4 = f32[4,2]{1,0:T(4,128)S(1)} collective-permute-done((f32[4,2]{1,0:T(4,128)S(1)}, f32[4,2]{1,0:T(4,128)S(1)}, u32[]{:S(2)}, u32[]{:S(2)}) %collective-permute-start.4) | collective-permute-done | bytes 64 | tf_op jit(solution)/shard_map/ppermute | solution.py:28
  169.8 2.4 %collective-permute-done.5 = f32[4,2]{1,0:T(4,128)S(1)} collective-permute-done((f32[4,2]{1,0:T(4,128)S(1)}, f32[4,2]{1,0:T(4,128)S(1)}, u32[]{:S(2)}, u32[]{:S(2)}) %collective-permute-start.5) | collective-permute-done | bytes 64 | tf_op jit(solution)/shard_map/ppermute | solution.py:28
  172.2 3.9 %collective-permute-done.6 = f32[4,2]{1,0:T(4,128)S(1)} collective-permute-done((f32[4,2]{1,0:T(4,128)S(1)}, f32[4,2]{1,0:T(4,128)S(1)}, u32[]{:S(2)}, u32[]{:S(2)}) %collective-permute-start.6) | collective-permute-done | bytes 64 | tf_op jit(solution)/shard_map/ppermute | solution.py:28
  176.1 3.0 %collective-permute-done.7 = f32[4,2]{1,0:T(4,128)S(1)} collective-permute-done((f32[4,2]{1,0:T(4,128)S(1)}, f32[4,2]{1,0:T(4,128)S(1)}, u32[]{:S(2)}, u32[]{:S(2)}) %collective-permute-start.7) | collective-permute-done | bytes 64 | tf_op jit(solution)/shard_map/ppermute | solution.py:28
  179.1 2.8 %collective-permute-done.8 = f32[4,2]{1,0:T(4,128)S(1)} collective-permute-done((f32[4,2]{1,0:T(4,128)S(1)}, f32[4,2]{1,0:T(4,128)S(1)}, u32[]{:S(2)}, u32[]{:S(2)}) %collective-permute-start.8) | collective-permute-done | bytes 64 | tf_op jit(solution)/shard_map/ppermute | solution.py:28
  182.0 4.3 %collective-permute-done.9 = f32[4,2]{1,0:T(4,128)S(1)} collective-permute-done((f32[4,2]{1,0:T(4,128)S(1)}, f32[4,2]{1,0:T(4,128)S(1)}, u32[]{:S(2)}, u32[]{:S(2)}) %collective-permute-start.9) | collective-permute-done | bytes 64 | tf_op jit(solution)/shard_map/ppermute | solution.py:28
  186.3 0.7 fusion.115
  187.0 14.8 %reduce-scatter.2.cloned.1.call-done = f32[2,1024,128]{2,1,0:T(8,128)} async-done(((f32[2,4096,128]{2,1,0:T(8,128)}), f32[2,1024,128]{2,1,0:T(8,128)}) %reduce-scatter.2.cloned.1.call-update) | async-done | bytes 1048592 | tf_op jit(solution)/shard_map/reduce_scatter | solution.py:113
  201.8 2.2 %slice_bitcast_fusion.2 = (f32[1024,128]{1,0:T(8,128)}, f32[1024,128]{1,0:T(8,128)}) fusion(f32[2,1024,128]{2,1,0:T(8,128)} %reduce-scatter.2.cloned.1.call-done), kind=kLoop, calls=%fused_computation.112 | loop fusion | bytes 2097152 | tf_op jit(solution)/shard_map/squeeze | solution.py:116
  (73 shorter events, 8.0 us)
Async XLA Ops:
  7.2 2.4 %copy-start.8 = (s32[128]{0:T(128)S(1)}, s32[128]{0:T(128)}, u32[]{:S(2)}) copy-start(s32[128]{0:T(128)} %param.9) | copy-start | bytes 1540
  7.2 4.5 %copy-start.7 = (s32[4,16,4]{1,2,0:T(4,128)S(1)}, s32[4,16,4]{1,2,0:T(4,128)}, u32[]{:S(2)}) copy-start(s32[4,16,4]{1,2,0:T(4,128)} %param.8) | copy-start | bytes 3076
  7.2 44.8 %all-gather.2.cloned.1.call-start = ((), (), s32[]{:S(2)}) async-start(), calls=%async_computation.1 | async-start | bytes 5242880 | tf_op jit(solution)/shard_map/all_gather | solution.py:80
  9.6 192.3 %reduce-scatter.2.cloned.1.call-start = ((), (), s32[]{:S(2)}) async-start(), calls=%async_computation.2 | async-start | bytes 5242880 | tf_op jit(solution)/shard_map/reduce_scatter | solution.py:113
  52.0 4.7 %slice-start = ((s8[8388608]{0:T(1024)(128)(4,1)}), s8[4194304]{0:T(1024)(128)(4,1)S(1)}, s32[]{:S(2)}) async-start(s8[8388608]{0:T(1024)(128)(4,1)} %bitcast.238), calls=%async_computation.3 | async-start | bytes 8388608
  53.8 3.1 %slice-start.1 = ((s8[8388608]{0:T(1024)(128)(4,1)}), s8[4194304]{0:T(1024)(128)(4,1)S(1)}, s32[]{:S(2)}) async-start(s8[8388608]{0:T(1024)(128)(4,1)} %bitcast.238), calls=%async_computation.4 | async-start | bytes 8388608
  56.0 6.4 %copy-start = (f32[2,2048,128]{2,1,0:T(8,128)}, f32[2,2048,128]{2,1,0:T(8,128)S(1)}, u32[]{:S(2)}) copy-start(f32[2,2048,128]{2,1,0:T(8,128)S(1)} %fusion.32) | copy-start | bytes 6291460
  56.0 1.4 copy-start.5
  59.2 0.9 copy-start.6
  60.2 2.3 %copy-start.1 = (f32[2048,128]{1,0:T(8,128)}, f32[2048,128]{1,0:T(8,128)S(1)}, u32[]{:S(2)}) copy-start(f32[2048,128]{1,0:T(8,128)S(1)} %get-tuple-element.54) | copy-start | bytes 3145732
  66.5 6.5 %collective-permute-start = (f32[2,512,128]{2,1,0:T(8,128)}, f32[2,512,128]{2,1,0:T(8,128)}, u32[]{:S(2)}, u32[]{:S(2)}) collective-permute-start(f32[2,512,128]{2,1,0:T(8,128)} %pad_maximum_fusion.1), channel_id=1, source_target_pairs={{0,1},{1,2},{2,3},{3,4},{4,5},{5,6},{6,7},{7,8},{8,9},{9,10},{10,1... | collective-permute-start | bytes 1572872 | tf_op jit(solution)/shard_map/ppermute | solution.py:18
  73.6 7.3 %slice-start.2 = ((s8[8388608]{0:T(1024)(128)(4,1)}), s8[4194304]{0:T(1024)(128)(4,1)S(1)}, s32[]{:S(2)}) async-start(s8[8388608]{0:T(1024)(128)(4,1)} %bitcast.240), calls=%async_computation.5 | async-start | bytes 8388608
  77.3 3.6 %slice-start.3 = ((s8[8388608]{0:T(1024)(128)(4,1)}), s8[4194304]{0:T(1024)(128)(4,1)S(1)}, s32[]{:S(2)}) async-start(s8[8388608]{0:T(1024)(128)(4,1)} %bitcast.240), calls=%async_computation.6 | async-start | bytes 8388608
  88.4 10.4 %collective-permute-start.1 = (f32[2,512,128]{2,1,0:T(8,128)}, f32[2,512,128]{2,1,0:T(8,128)}, u32[]{:S(2)}, u32[]{:S(2)}) collective-permute-start(f32[2,512,128]{2,1,0:T(8,128)} %pad_maximum_fusion.2), channel_id=1, source_target_pairs={{0,1},{1,2},{2,3},{3,4},{4,5},{5,6},{6,7},{7,8},{8,9},{9,10},{10,1... | collective-permute-start | bytes 1572872 | tf_op jit(solution)/shard_map/ppermute | solution.py:18
  99.4 7.4 %slice-start.4 = ((s8[8388608]{0:T(1024)(128)(4,1)}), s8[4194304]{0:T(1024)(128)(4,1)S(1)}, s32[]{:S(2)}) async-start(s8[8388608]{0:T(1024)(128)(4,1)} %bitcast.242), calls=%async_computation.7 | async-start | bytes 8388608
  103.1 1.9 copy-start.2
  103.1 3.7 %slice-start.5 = ((s8[8388608]{0:T(1024)(128)(4,1)}), s8[4194304]{0:T(1024)(128)(4,1)S(1)}, s32[]{:S(2)}) async-start(s8[8388608]{0:T(1024)(128)(4,1)} %bitcast.242), calls=%async_computation.8 | async-start | bytes 8388608
  106.8 1.0 copy-start.3
  114.6 13.8 %collective-permute-start.2 = (f32[2,512,128]{2,1,0:T(8,128)}, f32[2,512,128]{2,1,0:T(8,128)}, u32[]{:S(2)}, u32[]{:S(2)}) collective-permute-start(f32[2,512,128]{2,1,0:T(8,128)} %pad_maximum_fusion.3), channel_id=1, source_target_pairs={{0,1},{1,2},{2,3},{3,4},{4,5},{5,6},{6,7},{7,8},{8,9},{9,10},{10,1... | collective-permute-start | bytes 1572872 | tf_op jit(solution)/shard_map/ppermute | solution.py:18
  129.0 7.4 %slice-start.6 = ((s8[8388608]{0:T(1024)(128)(4,1)}), s8[4194304]{0:T(1024)(128)(4,1)S(1)}, s32[]{:S(2)}) async-start(s8[8388608]{0:T(1024)(128)(4,1)} %bitcast.244), calls=%async_computation.9 | async-start | bytes 8388608
  132.7 3.7 %slice-start.7 = ((s8[8388608]{0:T(1024)(128)(4,1)}), s8[4194304]{0:T(1024)(128)(4,1)S(1)}, s32[]{:S(2)}) async-start(s8[8388608]{0:T(1024)(128)(4,1)} %bitcast.244), calls=%async_computation.10 | async-start | bytes 8388608
  134.6 3.3 %copy-start.4 = (f32[512,128]{1,0:T(8,128)}, f32[512,128]{1,0:T(8,128)S(1)}, u32[]{:S(2)}) copy-start(f32[512,128]{1,0:T(8,128)S(1)} %get-tuple-element.76) | copy-start | bytes 786436
  150.2 15.4 %collective-permute-start.3 = (f32[4,2]{1,0:T(4,128)S(1)}, f32[4,2]{1,0:T(4,128)S(1)}, u32[]{:S(2)}, u32[]{:S(2)}) collective-permute-start(f32[4,2]{1,0:T(4,128)S(1)} %pad_maximum_fusion.4), channel_id=1, source_target_pairs={{0,1},{1,0},{2,3},{3,2},{4,5},{5,4},{6,7},{7,6},{8,9},{9,8},{10,11... | collective-permute-start | bytes 104 | tf_op jit(solution)/shard_map/ppermute | solution.py:28
  165.6 4.0 %collective-permute-start.4 = (f32[4,2]{1,0:T(4,128)S(1)}, f32[4,2]{1,0:T(4,128)S(1)}, u32[]{:S(2)}, u32[]{:S(2)}) collective-permute-start(f32[4,2]{1,0:T(4,128)S(1)} %fusion.118), channel_id=1, source_target_pairs={{0,2},{1,3},{2,0},{3,1},{4,6},{5,7},{6,4},{7,5},{8,10},{9,11},{10,... | collective-permute-start | bytes 104 | tf_op jit(solution)/shard_map/ppermute | solution.py:28
  169.7 2.5 %collective-permute-start.5 = (f32[4,2]{1,0:T(4,128)S(1)}, f32[4,2]{1,0:T(4,128)S(1)}, u32[]{:S(2)}, u32[]{:S(2)}) collective-permute-start(f32[4,2]{1,0:T(4,128)S(1)} %fusion.151), channel_id=1, source_target_pairs={{0,4},{1,5},{2,6},{3,7},{4,0},{5,1},{6,2},{7,3},{8,12},{9,13},{10,... | collective-permute-start | bytes 104 | tf_op jit(solution)/shard_map/ppermute | solution.py:28
  172.2 3.9 %collective-permute-start.6 = (f32[4,2]{1,0:T(4,128)S(1)}, f32[4,2]{1,0:T(4,128)S(1)}, u32[]{:S(2)}, u32[]{:S(2)}) collective-permute-start(f32[4,2]{1,0:T(4,128)S(1)} %add.226), channel_id=1, source_target_pairs={{0,8},{1,9},{2,10},{3,11},{4,12},{5,13},{6,14},{7,15},{8,0},{9,1},... | collective-permute-start | bytes 104 | tf_op jit(solution)/shard_map/ppermute | solution.py:28
  176.1 3.0 %collective-permute-start.7 = (f32[4,2]{1,0:T(4,128)S(1)}, f32[4,2]{1,0:T(4,128)S(1)}, u32[]{:S(2)}, u32[]{:S(2)}) collective-permute-start(f32[4,2]{1,0:T(4,128)S(1)} %add.227), channel_id=1, source_target_pairs={{0,16},{1,17},{2,18},{3,19},{4,20},{5,21},{6,22},{7,23},{8,24},{9,... | collective-permute-start | bytes 104 | tf_op jit(solution)/shard_map/ppermute | solution.py:28
  179.1 2.8 %collective-permute-start.8 = (f32[4,2]{1,0:T(4,128)S(1)}, f32[4,2]{1,0:T(4,128)S(1)}, u32[]{:S(2)}, u32[]{:S(2)}) collective-permute-start(f32[4,2]{1,0:T(4,128)S(1)} %add.228), channel_id=1, source_target_pairs={{0,32},{1,33},{2,34},{3,35},{4,36},{5,37},{6,38},{7,39},{8,40},{9,... | collective-permute-start | bytes 104 | tf_op jit(solution)/shard_map/ppermute | solution.py:28
  182.0 4.3 %collective-permute-start.9 = (f32[4,2]{1,0:T(4,128)S(1)}, f32[4,2]{1,0:T(4,128)S(1)}, u32[]{:S(2)}, u32[]{:S(2)}) collective-permute-start(f32[4,2]{1,0:T(4,128)S(1)} %add.229), channel_id=1, source_target_pairs={{0,64},{1,65},{2,66},{3,67},{4,68},{5,69},{6,70},{7,71},{8,72},{9,... | collective-permute-start | bytes 104 | tf_op jit(solution)/shard_map/ppermute | solution.py:28
Sparse Core Ops, SparseCore 0:
  9.7 42.2 all-gather.1
  145.0 56.7 reduce-scatter.1

commit v3 on v2

--- a/solution.py
+++ b/solution.py
@@ -2,6 +2,8 @@
 import jax.numpy as jnp
 from jax import lax
 from jax.sharding import PartitionSpec as P
+from jax.experimental import pallas as pl
+from jax.experimental.pallas import tpu as pltpu
 
 TILE = 128
 UT = 8
@@ -63,6 +65,93 @@
     return (user_fac, user_acc, item_fac, item_acc, sq_error)
 
 
+CHUNK = 128
+
+
+def stratum_kernel(
+    mask_ref, rating_ref, u_in, gu_in, v_in, gv_in, u_ref, gu_ref, v_ref, gv_ref, sq_ref, gv_acc
+):
+    row_count = u_ref.shape[0]
+    item_count = v_ref.shape[0]
+    user_scale = float(item_count) ** (-0.5)
+    item_scale = float(UT * TILE) ** (-0.5)
+    u_ref[...] = u_in[...]
+    gu_ref[...] = gu_in[...]
+    v_ref[...] = v_in[...]
+    gv_ref[...] = gv_in[...]
+    sq_ref[...] = jnp.zeros(sq_ref.shape, jnp.float32)
+    for inner in range(STEPS):
+        item_half = v_ref[...].astype(jnp.bfloat16)
+        gv_acc[...] = jnp.zeros(gv_acc.shape, jnp.float32)
+
+        def body(chunk, carry, inner=inner, item_half=item_half):
+            rows = pl.ds(pl.multiple_of(chunk * CHUNK, CHUNK), CHUNK)
+            user_fac = u_ref[rows, :]
+            user_acc = gu_ref[rows, :]
+            user_half = user_fac.astype(jnp.bfloat16)
+            predicted = lax.dot_general(
+                user_half, item_half, (((1,), (1,)), ((), ())), preferred_element_type=jnp.float32
+            )
+            residue = predicted - rating_ref[rows, :].astype(jnp.float32)
+            masked = residue * mask_ref[pl.ds(chunk, 1), :]
+            if inner == 0:
+                sq_ref[...] += jnp.sum(masked * residue, axis=0, keepdims=True)
+            err_half = masked.astype(jnp.bfloat16)
+            grad_user = (
+                jnp.dot(err_half, item_half, preferred_element_type=jnp.float32) * user_scale
+                + ridge_weight * user_fac
+            )
+            gv_acc[...] += lax.dot_general(
+                err_half, user_half, (((0,), (0,)), ((), ())), preferred_element_type=jnp.float32
+            )
+            user_acc = user_acc + grad_user * grad_user
+            u_ref[rows, :] = user_fac - step_rate * grad_user * lax.rsqrt(user_acc)
+            gu_ref[rows, :] = user_acc
+            return carry
+
+        lax.fori_loop(0, row_count // CHUNK, body, 0)
+        item_fac = v_ref[...]
+        grad_item = gv_acc[...] * item_scale + ridge_weight * item_fac
+        item_acc = gv_ref[...] + grad_item * grad_item
+        gv_ref[...] = item_acc
+        v_ref[...] = item_fac - step_rate * grad_item * lax.rsqrt(item_acc)
+
+
+def run_stratum(stratum, ratings, mask_rows, user_fac, user_acc, item_fac, item_acc):
+    rows, rank = user_fac.shape
+    items_here = item_fac.shape[0]
+    whole = lambda shape: pl.BlockSpec(shape, lambda i: (0,) * len(shape))
+    outs = pl.pallas_call(
+        stratum_kernel,
+        grid=(1,),
+        in_specs=[
+            whole(mask_rows.shape),
+            pl.BlockSpec((None, rows, items_here), lambda i: (stratum, 0, 0)),
+            whole((rows, rank)),
+            whole((rows, rank)),
+            whole((items_here, rank)),
+            whole((items_here, rank)),
+        ],
+        out_specs=[
+            whole((rows, rank)),
+            whole((rows, rank)),
+            whole((items_here, rank)),
+            whole((items_here, rank)),
+            whole((1, items_here)),
+        ],
+        out_shape=[
+            jax.ShapeDtypeStruct((rows, rank), jnp.float32),
+            jax.ShapeDtypeStruct((rows, rank), jnp.float32),
+            jax.ShapeDtypeStruct((items_here, rank), jnp.float32),
+            jax.ShapeDtypeStruct((items_here, rank), jnp.float32),
+            jax.ShapeDtypeStruct((1, items_here), jnp.float32),
+        ],
+        scratch_shapes=[pltpu.VMEM((items_here, rank), jnp.float32)],
+        input_output_aliases={2: 0, 3: 1, 4: 2, 5: 3},
+    )(mask_rows, ratings, user_fac, user_acc, item_fac, item_acc)
+    return outs[0], outs[1], outs[2], outs[3], jnp.sum(outs[4])
+
+
 def on_device(ratings, tile_mask, tile_counts, users, user_accum, items, item_accum):
     strata_count = ratings.shape[0]
     slot_count = tile_mask.shape[1]
@@ -83,22 +172,21 @@
     user_pair = lax.dynamic_slice_in_dim(ext_pair, start_tile * tile_size, pad_rows, 1)
     user_fac = user_pair[0]
     user_acc = user_pair[1]
-    held_pair = jnp.stack([items, item_accum])
     loss_list = []
+    item_fac = items
+    item_acc = item_accum
     for stratum in range(strata_count):
         live_tiles = tile_mask[stratum].astype(jnp.float32) * valid[:, None]
-        item_fac = held_pair[0]
-        item_acc = held_pair[1]
-        for inner in range(STEPS):
-            user_fac, user_acc, item_fac, item_acc, sq_error = update(
-                user_fac, user_acc, item_fac, item_acc, ratings[stratum], live_tiles
-            )
-            if inner == 0:
-                observed = jnp.sum(live_tiles) * float(tile_size * tile_size)
-                loss_list.append(jnp.stack([sq_error, observed]))
-        held_pair = jnp.stack([item_fac, item_acc])
+        mask_rows = jnp.repeat(live_tiles, tile_size, axis=1)
+        user_fac, user_acc, item_fac, item_acc, sq_error = run_stratum(
+            stratum, ratings, mask_rows, user_fac, user_acc, item_fac, item_acc
+        )
+        observed = jnp.sum(live_tiles) * float(tile_size * tile_size)
+        loss_list.append(jnp.stack([sq_error, observed]))
         if stratum + 1 < strata_count:
-            held_pair = passed_along(held_pair, ("row", "col"), 1)
+            held_pair = passed_along(jnp.stack([item_fac, item_acc]), ("row", "col"), 1)
+            item_fac = held_pair[0]
+            item_acc = held_pair[1]
     loss_parts = butterfly_sum(jnp.stack(loss_list), ("row", "col"))
     losses = loss_parts[:, 0] / loss_parts[:, 1]
     row_valid = jnp.repeat(valid, tile_size)[None, :, None] > 0.5
@@ -113,7 +201,7 @@
     users_pair = lax.psum_scatter(
         frame_pair[:, : group_size * arrived_rows], "col", scatter_dimension=1, tiled=True
     )
-    return (users_pair[0], users_pair[1], held_pair[0], held_pair[1], losses)
+    return (users_pair[0], users_pair[1], item_fac, item_acc, losses)
 
 
 def solution(mesh):

time: 211 us -> 262 us (1.24)
  Pallas kernels: 0 us -> 95.1 us
  matrix products: 55.9 us -> 0 us
  local copies, waits for them, and re-layouts: 10.8 us -> 18.1 us
  waiting for transfers between devices: 90.4 us -> 93.6 us
    pallas_call x0 -> x4, Pallas kernels: none -> 95.1 us  [run_stratum(): pl.pallas_call(stratum_kernel, grid=(1,), in_specs=[whole(mask_rows.shape...]
    dot_general x36 -> x0, matrix products: 55.9 us -> none  [the longest x12 19.2 us: update(): jnp.dot(err_half, item_half, preferred_element_type=jnp.float32)]
    unnamed x34 -> x22, local copies, waits for them, and re-layouts: 1.25 us -> 7 us
    squeeze x1 -> x5, local copies, waits for them, and re-layouts: 2.23 us -> 6.17 us  [the longest x3 2.47 us: on_device(): item_acc = held_pair[1]]
    ppermute x3, waiting for transfers between devices: 15.6 us -> 19.3 us  [passed_along(): return lax.ppermute(value, axis, pairs)]
  transfers between devices with their start and end apart: 12 -> 12, of which waited for: 11 -> 12; matrix products, arithmetic and copies ran while one was open for 7% -> 4% of each run, Pallas kernels for 0% -> 0%
where the time goes in v3:
time: 262 us; the launch traced here: 261 us
  Pallas kernels  95.1 us (36%)
  waiting for transfers between devices  93.6 us (36%)
  starting transfers between devices  21.2 us (8%)
  local copies, waits for them, and re-layouts  18.1 us (7%)
  between operations  17.3 us (7%)
  other arithmetic  16 us (6%)
    pallas_call x4, Pallas kernels, run_stratum(): pl.pallas_call(stratum_kernel, grid=(1,), in_specs=[whole(mask_rows.shape...  95.1 us
    all_gather x1, waiting for transfers between devices, on_device(): lax.all_gather(jnp.stack([users, user_accum]), 'col', axis=1, tiled=True)  38.8 us
    ppermute x7, waiting for transfers between devices, butterfly_sum(): value = value + lax.ppermute(value, axis, pairs)  21.3 us
    ppermute x3, waiting for transfers between devices, passed_along(): return lax.ppermute(value, axis, pairs)  19.3 us
    reduce_scatter x1, waiting for transfers between devices, on_device(): lax.psum_scatter(frame_pair[:, :group_size * arrived_rows], 'col', scatte...  14.2 us
    ppermute x7, starting transfers between devices, butterfly_sum(): value = value + lax.ppermute(value, axis, pairs)  12.9 us
    ppermute x3, starting transfers between devices, passed_along(): return lax.ppermute(value, axis, pairs)  8.22 us
    unnamed x22, local copies, waits for them, and re-layouts  7 us
  transfers between devices with their start and end apart: 12, of which 12 were waited for; matrix products, arithmetic and copies ran while one was open for 4% of the time, Pallas kernels for 0%

profile of v3, /device:TPU:1, one launch (start us, length us, event | category | flops | bytes accessed | tf_op | source)
XLA Modules:
  0.0 261.3 jit_solution(2730035064015643367)
XLA Ops:
  7.2 1.7 copy.67.v_in
  8.9 1.7 copy.68.gv_in
  10.6 2.2 pad_maximum_fusion
  12.9 0.7 fusion.3
  14.3 0.7 compare_convert_fusion
  14.9 0.7 fusion.6
  15.6 0.1 copy.35
  15.7 0.1 broadcast_in_dim.46
  15.8 0.6 copy.44
  16.4 38.8 %all-gather.2.cloned.1.call-done = f32[2,4096,128]{2,1,0:T(8,128)} async-done(((f32[2,1024,128]{2,1,0:T(8,128)}), f32[2,4096,128]{2,1,0:T(8,128)}) %all-gather.2.cloned.1.call-update) | async-done | bytes 4194320 | tf_op jit(solution)/shard_map/all_gather | solution.py:169
  55.2 1.6 slice-done
  56.8 2.0 fusion
  58.8 1.5 slice_bitcast_fusion
  60.3 23.8 %shard_map.110 = (f32[2048,128]{1,0:T(8,128)}, f32[2048,128]{1,0:T(8,128)}, f32[512,128]{1,0:T(8,128)}, f32[512,128]{1,0:T(8,128)}, f32[1,512]{1,0:T(1,128)}) custom-call(f32[16,512]{1,0:T(8,128)} %bitcast.86, bf16[4,2048,512]{2,1,0:T(8,128)(2,1)} %rating_ref.7, ...), custom_call_target="tpu_custom_call", output_to_operand_aliasing={{0}: (2, {}), {1}: (3, {}), {2}: (4, {}), {3}: (5, {})} | custom-call | tf_op jit(solution)/shard_map/pallas_call | solution.py:124
  84.1 1.1 pad_maximum_fusion.1
  85.2 0.1 collective-permute-start
  85.3 0.1 copy.34
  85.4 0.1 broadcast_in_dim.45
  85.4 0.6 copy.45
  86.1 5.3 %collective-permute-done = f32[2,512,128]{2,1,0:T(8,128)S(1)} collective-permute-done((f32[2,512,128]{2,1,0:T(8,128)S(1)}, f32[2,512,128]{2,1,0:T(8,128)S(1)}, u32[]{:S(2)}, u32[]{:S(2)}) %collective-permute-start) | collective-permute-done | bytes 524320 | tf_op jit(solution)/shard_map/ppermute | solution.py:20
  91.4 0.8 slice_bitcast_fusion.8
  92.2 23.8 %shard_map.111 = (f32[2048,128]{1,0:T(8,128)}, f32[2048,128]{1,0:T(8,128)}, f32[512,128]{1,0:T(8,128)}, f32[512,128]{1,0:T(8,128)}, f32[1,512]{1,0:T(1,128)}) custom-call(f32[16,512]{1,0:T(8,128)} %bitcast.88, bf16[4,2048,512]{2,1,0:T(8,128)(2,1)} %rating_ref.7, ...), custom_call_target="tpu_custom_call", output_to_operand_aliasing={{0}: (2, {}), {1}: (3, {}), {2}: (4, {}), {3}: (5, {})} | custom-call | tf_op jit(solution)/shard_map/pallas_call | solution.py:124
  116.0 1.1 pad_maximum_fusion.2
  117.1 4.0 %collective-permute-start.1 = (f32[2,512,128]{2,1,0:T(8,128)S(1)}, f32[2,512,128]{2,1,0:T(8,128)S(1)}, u32[]{:S(2)}, u32[]{:S(2)}) collective-permute-start(f32[2,512,128]{2,1,0:T(8,128)S(1)} %pad_maximum_fusion.2), channel_id=1, source_target_pairs={{0,1},{1,2},{2,3},{3,4},{4,5},{5,6},{6,7},{7,8},{8,9},{9,10},{10,1... | collective-permute-start | bytes 1572872 | tf_op jit(solution)/shard_map/ppermute | solution.py:20
  121.1 0.1 copy.33
  121.2 0.1 broadcast_in_dim.44
  121.3 0.6 copy.46
  121.9 5.3 %collective-permute-done.1 = f32[2,512,128]{2,1,0:T(8,128)S(1)} collective-permute-done((f32[2,512,128]{2,1,0:T(8,128)S(1)}, f32[2,512,128]{2,1,0:T(8,128)S(1)}, u32[]{:S(2)}, u32[]{:S(2)}) %collective-permute-start.1) | collective-permute-done | bytes 524320 | tf_op jit(solution)/shard_map/ppermute | solution.py:20
  127.2 0.8 slice_bitcast_fusion.6
  128.1 23.8 %shard_map.112 = (f32[2048,128]{1,0:T(8,128)}, f32[2048,128]{1,0:T(8,128)}, f32[512,128]{1,0:T(8,128)}, f32[512,128]{1,0:T(8,128)}, f32[1,512]{1,0:T(1,128)}) custom-call(f32[16,512]{1,0:T(8,128)} %bitcast.89, bf16[4,2048,512]{2,1,0:T(8,128)(2,1)} %rating_ref.7, ...), custom_call_target="tpu_custom_call", output_to_operand_aliasing={{0}: (2, {}), {1}: (3, {}), {2}: (4, {}), {3}: (5, {})} | custom-call | tf_op jit(solution)/shard_map/pallas_call | solution.py:124
  151.8 1.1 pad_maximum_fusion.3
  152.9 4.0 %collective-permute-start.2 = (f32[2,512,128]{2,1,0:T(8,128)S(1)}, f32[2,512,128]{2,1,0:T(8,128)S(1)}, u32[]{:S(2)}, u32[]{:S(2)}) collective-permute-start(f32[2,512,128]{2,1,0:T(8,128)S(1)} %pad_maximum_fusion.3), channel_id=1, source_target_pairs={{0,1},{1,2},{2,3},{3,4},{4,5},{5,6},{6,7},{7,8},{8,9},{9,10},{10,1... | collective-permute-start | bytes 1572872 | tf_op jit(solution)/shard_map/ppermute | solution.py:20
  156.9 0.1 copy.32
  157.0 0.1 broadcast_in_dim.43
  157.1 0.6 copy.47
  157.8 8.6 %collective-permute-done.2 = f32[2,512,128]{2,1,0:T(8,128)S(1)} collective-permute-done((f32[2,512,128]{2,1,0:T(8,128)S(1)}, f32[2,512,128]{2,1,0:T(8,128)S(1)}, u32[]{:S(2)}, u32[]{:S(2)}) %collective-permute-start.2) | collective-permute-done | bytes 524320 | tf_op jit(solution)/shard_map/ppermute | solution.py:20
  166.4 0.8 slice_bitcast_fusion.4
  167.2 23.8 %shard_map.113 = (f32[2048,128]{1,0:T(8,128)}, f32[2048,128]{1,0:T(8,128)}, f32[512,128]{1,0:T(8,128)}, f32[512,128]{1,0:T(8,128)}, f32[1,512]{1,0:T(1,128)}) custom-call(f32[16,512]{1,0:T(8,128)} %bitcast.87, bf16[4,2048,512]{2,1,0:T(8,128)(2,1)} %rating_ref.7, ...), custom_call_target="tpu_custom_call", output_to_operand_aliasing={{0}: (2, {}), {1}: (3, {}), {2}: (4, {}), {3}: (5, {})} | custom-call | tf_op jit(solution)/shard_map/pallas_call | solution.py:124
  191.0 0.4 broadcast_in_dim.39
  191.4 0.8 copy-done
  192.2 0.3 copy-done.1
  192.6 0.4 fusion.1
  193.0 2.2 slice.81
  197.7 0.6 reduce_sum.92
  198.3 0.7 maximum_bitcast_fusion
  199.1 0.6 reduce_sum.94
  199.7 0.7 maximum_bitcast_fusion.1
  200.4 0.6 reduce_sum.96
  201.0 0.7 maximum_bitcast_fusion.2
  201.7 0.6 reduce_sum.98
  202.3 0.7 maximum_bitcast_fusion.3
  203.0 12.7 %collective-permute-start.3 = (f32[4,2]{1,0:T(4,128)S(1)}, f32[4,2]{1,0:T(4,128)S(1)}, u32[]{:S(2)}, u32[]{:S(2)}) collective-permute-start(f32[4,2]{1,0:T(4,128)S(1)} %pad_maximum_fusion.4), channel_id=1, source_target_pairs={{0,1},{1,0},{2,3},{3,2},{4,5},{5,4},{6,7},{7,6},{8,9},{9,8},{10,11... | collective-permute-start | bytes 104 | tf_op jit(solution)/shard_map/ppermute | solution.py:30
  215.8 0.8 collective-permute-done.3
  216.6 0.1 collective-permute-start.4
  216.7 3.9 %collective-permute-done.4 = f32[4,2]{1,0:T(4,128)S(1)} collective-permute-done((f32[4,2]{1,0:T(4,128)S(1)}, f32[4,2]{1,0:T(4,128)S(1)}, u32[]{:S(2)}, u32[]{:S(2)}) %collective-permute-start.4) | collective-permute-done | bytes 64 | tf_op jit(solution)/shard_map/ppermute | solution.py:30
  220.7 0.1 collective-permute-start.5
  220.8 2.4 collective-permute-done.5
  223.2 3.9 %collective-permute-done.6 = f32[4,2]{1,0:T(4,128)S(1)} collective-permute-done((f32[4,2]{1,0:T(4,128)S(1)}, f32[4,2]{1,0:T(4,128)S(1)}, u32[]{:S(2)}, u32[]{:S(2)}) %collective-permute-start.6) | collective-permute-done | bytes 64 | tf_op jit(solution)/shard_map/ppermute | solution.py:30
  227.1 3.0 %collective-permute-done.7 = f32[4,2]{1,0:T(4,128)S(1)} collective-permute-done((f32[4,2]{1,0:T(4,128)S(1)}, f32[4,2]{1,0:T(4,128)S(1)}, u32[]{:S(2)}, u32[]{:S(2)}) %collective-permute-start.7) | collective-permute-done | bytes 64 | tf_op jit(solution)/shard_map/ppermute | solution.py:30
  230.1 2.8 %collective-permute-done.8 = f32[4,2]{1,0:T(4,128)S(1)} collective-permute-done((f32[4,2]{1,0:T(4,128)S(1)}, f32[4,2]{1,0:T(4,128)S(1)}, u32[]{:S(2)}, u32[]{:S(2)}) %collective-permute-start.8) | collective-permute-done | bytes 64 | tf_op jit(solution)/shard_map/ppermute | solution.py:30
  233.0 4.3 %collective-permute-done.9 = f32[4,2]{1,0:T(4,128)S(1)} collective-permute-done((f32[4,2]{1,0:T(4,128)S(1)}, f32[4,2]{1,0:T(4,128)S(1)}, u32[]{:S(2)}, u32[]{:S(2)}) %collective-permute-start.9) | collective-permute-done | bytes 64 | tf_op jit(solution)/shard_map/ppermute | solution.py:30
  237.3 0.7 fusion.2
  238.0 14.2 %reduce-scatter.2.cloned.1.call-done = f32[2,1024,128]{2,1,0:T(8,128)} async-done(((f32[2,4096,128]{2,1,0:T(8,128)}), f32[2,1024,128]{2,1,0:T(8,128)}) %reduce-scatter.2.cloned.1.call-update) | async-done | bytes 1048592 | tf_op jit(solution)/shard_map/reduce_scatter | solution.py:201
  252.2 2.2 slice_bitcast_fusion.2
  (32 shorter events, 0.3 us)
Async XLA Ops:
  7.2 7.8 %copy-start.2 = (s32[4,16,4]{1,2,0:T(4,128)S(1)}, s32[4,16,4]{1,2,0:T(4,128)}, u32[]{:S(2)}) copy-start(s32[4,16,4]{1,2,0:T(4,128)} %param.8) | copy-start | bytes 3076
  7.2 5.7 %copy-start.7 = (s32[128]{0:T(128)S(1)}, s32[128]{0:T(128)}, u32[]{:S(2)}) copy-start(s32[128]{0:T(128)} %param.9) | copy-start | bytes 1540
  7.2 48.1 %all-gather.2.cloned.1.call-start = ((), (), s32[]{:S(2)}) async-start(), calls=%async_computation.1 | async-start | bytes 5242880 | tf_op jit(solution)/shard_map/all_gather | solution.py:169
  12.8 239.4 %reduce-scatter.2.cloned.1.call-start = ((), (), s32[]{:S(2)}) async-start(), calls=%async_computation.2 | async-start | bytes 5242880 | tf_op jit(solution)/shard_map/reduce_scatter | solution.py:201
  55.2 1.6 slice-start
  85.2 6.2 %collective-permute-start = (f32[2,512,128]{2,1,0:T(8,128)S(1)}, f32[2,512,128]{2,1,0:T(8,128)S(1)}, u32[]{:S(2)}, u32[]{:S(2)}) collective-permute-start(f32[2,512,128]{2,1,0:T(8,128)S(1)} %pad_maximum_fusion.1), channel_id=1, source_target_pairs={{0,1},{1,2},{2,3},{3,4},{4,5},{5,6},{6,7},{7,8},{8,9},{9,10},{10,1... | collective-permute-start | bytes 1572872 | tf_op jit(solution)/shard_map/ppermute | solution.py:20
  117.1 10.2 %collective-permute-start.1 = (f32[2,512,128]{2,1,0:T(8,128)S(1)}, f32[2,512,128]{2,1,0:T(8,128)S(1)}, u32[]{:S(2)}, u32[]{:S(2)}) collective-permute-start(f32[2,512,128]{2,1,0:T(8,128)S(1)} %pad_maximum_fusion.2), channel_id=1, source_target_pairs={{0,1},{1,2},{2,3},{3,4},{4,5},{5,6},{6,7},{7,8},{8,9},{9,10},{10,1... | collective-permute-start | bytes 1572872 | tf_op jit(solution)/shard_map/ppermute | solution.py:20
  152.9 13.5 %collective-permute-start.2 = (f32[2,512,128]{2,1,0:T(8,128)S(1)}, f32[2,512,128]{2,1,0:T(8,128)S(1)}, u32[]{:S(2)}, u32[]{:S(2)}) collective-permute-start(f32[2,512,128]{2,1,0:T(8,128)S(1)} %pad_maximum_fusion.3), channel_id=1, source_target_pairs={{0,1},{1,2},{2,3},{3,4},{4,5},{5,6},{6,7},{7,8},{8,9},{9,10},{10,1... | collective-permute-start | bytes 1572872 | tf_op jit(solution)/shard_map/ppermute | solution.py:20
  191.0 1.2 copy-start
  191.0 1.5 copy-start.1
  195.2 2.5 copy-start.3
  195.2 3.8 %copy-start.4 = (f32[1,512]{1,0:T(1,128)S(1)}, f32[1,512]{1,0:T(1,128)}, u32[]{:S(2)}) copy-start(f32[1,512]{1,0:T(1,128)} %get-tuple-element.42) | copy-start | bytes 6148
  195.2 5.2 %copy-start.5 = (f32[1,512]{1,0:T(1,128)S(1)}, f32[1,512]{1,0:T(1,128)}, u32[]{:S(2)}) copy-start(f32[1,512]{1,0:T(1,128)} %get-tuple-element.43) | copy-start | bytes 6148
  195.2 6.5 %copy-start.6 = (f32[1,512]{1,0:T(1,128)S(1)}, f32[1,512]{1,0:T(1,128)}, u32[]{:S(2)}) copy-start(f32[1,512]{1,0:T(1,128)} %get-tuple-element.44) | copy-start | bytes 6148
  203.0 13.6 %collective-permute-start.3 = (f32[4,2]{1,0:T(4,128)S(1)}, f32[4,2]{1,0:T(4,128)S(1)}, u32[]{:S(2)}, u32[]{:S(2)}) collective-permute-start(f32[4,2]{1,0:T(4,128)S(1)} %pad_maximum_fusion.4), channel_id=1, source_target_pairs={{0,1},{1,0},{2,3},{3,2},{4,5},{5,4},{6,7},{7,6},{8,9},{9,8},{10,11... | collective-permute-start | bytes 104 | tf_op jit(solution)/shard_map/ppermute | solution.py:30
  216.6 4.0 %collective-permute-start.4 = (f32[4,2]{1,0:T(4,128)S(1)}, f32[4,2]{1,0:T(4,128)S(1)}, u32[]{:S(2)}, u32[]{:S(2)}) collective-permute-start(f32[4,2]{1,0:T(4,128)S(1)} %fusion.5), channel_id=1, source_target_pairs={{0,2},{1,3},{2,0},{3,1},{4,6},{5,7},{6,4},{7,5},{8,10},{9,11},{10,... | collective-permute-start | bytes 104 | tf_op jit(solution)/shard_map/ppermute | solution.py:30
  220.7 2.5 collective-permute-start.5
  223.2 3.9 %collective-permute-start.6 = (f32[4,2]{1,0:T(4,128)S(1)}, f32[4,2]{1,0:T(4,128)S(1)}, u32[]{:S(2)}, u32[]{:S(2)}) collective-permute-start(f32[4,2]{1,0:T(4,128)S(1)} %add.34), channel_id=1, source_target_pairs={{0,8},{1,9},{2,10},{3,11},{4,12},{5,13},{6,14},{7,15},{8,0},{9,1},... | collective-permute-start | bytes 104 | tf_op jit(solution)/shard_map/ppermute | solution.py:30
  227.1 3.0 %collective-permute-start.7 = (f32[4,2]{1,0:T(4,128)S(1)}, f32[4,2]{1,0:T(4,128)S(1)}, u32[]{:S(2)}, u32[]{:S(2)}) collective-permute-start(f32[4,2]{1,0:T(4,128)S(1)} %add.35), channel_id=1, source_target_pairs={{0,16},{1,17},{2,18},{3,19},{4,20},{5,21},{6,22},{7,23},{8,24},{9,... | collective-permute-start | bytes 104 | tf_op jit(solution)/shard_map/ppermute | solution.py:30
  230.1 2.8 %collective-permute-start.8 = (f32[4,2]{1,0:T(4,128)S(1)}, f32[4,2]{1,0:T(4,128)S(1)}, u32[]{:S(2)}, u32[]{:S(2)}) collective-permute-start(f32[4,2]{1,0:T(4,128)S(1)} %add.36), channel_id=1, source_target_pairs={{0,32},{1,33},{2,34},{3,35},{4,36},{5,37},{6,38},{7,39},{8,40},{9,... | collective-permute-start | bytes 104 | tf_op jit(solution)/shard_map/ppermute | solution.py:30
  233.0 4.3 %collective-permute-start.9 = (f32[4,2]{1,0:T(4,128)S(1)}, f32[4,2]{1,0:T(4,128)S(1)}, u32[]{:S(2)}, u32[]{:S(2)}) collective-permute-start(f32[4,2]{1,0:T(4,128)S(1)} %add.37), channel_id=1, source_target_pairs={{0,64},{1,65},{2,66},{3,67},{4,68},{5,69},{6,70},{7,71},{8,72},{9,... | collective-permute-start | bytes 104 | tf_op jit(solution)/shard_map/ppermute | solution.py:30
Sparse Core Ops, SparseCore 0:
  13.0 42.2 all-gather.1
  195.4 56.7 reduce-scatter.1
